TPU v7x, 32 devices: a whole 2x2x4 slice. The times are simulated.
32 devices in a mesh: band: 16 (over z, x, core), chan: 2 (over y).
Axes of the slice: x: 2, y: 2, z: 4, core: 2. Of those that a mesh axis runs over, the one named last changes fastest.
Arguments:
- features: bfloat16 [256, 64, 1024], P('chan', 'band'), may hold values from -6 to 6
- depth_kernel: bfloat16 [3, 9, 256], P(None, None, 'chan'), may hold values from -2 to 2
- pointwise: bfloat16 [4, 256, 256], P(None, 'chan'), may hold values from -0.25 to 0.25
- cotangent: bfloat16 [256, 64, 1024], P('chan', 'band'), may hold values from -6 to 6
Outputs:
- output: bfloat16 [256, 64, 1024], P('chan', 'band')
- grad_input: float32 [256, 64, 1024], P('chan', 'band')
- grad_depth: float32 [3, 9, 256], P(None, None, 'chan')
- grad_point: float32 [4, 256, 256], P(None, 'chan')
All inputs are finite; a program needn't handle non-finite values.
Results may differ from a plain program's by a relative error of at most 0.0057.
Values may be sent and summed in bfloat16 or wider, within the bound.
No kernel may reach another device: no remote copies, remote signals or barrier semaphores. Data moves between devices by JAX's collectives and lax.ppermute only.
A program may use at most 128 MiB of HBM per device.

v0:
```python
import jax
import jax.numpy as jnp
from jax import lax
from jax.sharding import PartitionSpec as P


GSCALE = 1024


dilations = (6, 12, 18)


def shifted(block, axis, distance):
    devices = range(lax.axis_size(axis))
    route = [(i - distance, i) for i in devices if i - distance in devices]
    if not route:
        return jnp.zeros_like(block)
    return lax.ppermute(block, axis, route)


def pieces_of(height, offset):
    ahead, start = divmod(offset, height)
    if start == 0:
        return [(ahead, 0, height)]
    return [(ahead, start, height), (ahead + 1, 0, start)]


def halo_rows(requests):
    groups = {}
    for key, (field, offset) in requests.items():
        for ahead, first, last in pieces_of(field.shape[1], offset):
            groups.setdefault((ahead, last - first), []).append((key, field, first, last))
    got = {}
    for (ahead, rows), members in groups.items():
        blocks = [field[:, first:last] for _, field, first, last in members]
        joined = jnp.concatenate(blocks, axis=0) if len(blocks) > 1 else blocks[0]
        if ahead != 0:
            joined = shifted(joined, "band", -ahead)
        at = 0
        for (key, field, first, last), block in zip(members, blocks):
            got.setdefault(key, []).append((first, joined[at : at + block.shape[0]]))
            at += block.shape[0]
    out = {}
    for key, (field, offset) in requests.items():
        parts = got[key]
        out[key] = parts[0][1] if len(parts) == 1 else jnp.concatenate([p for _, p in parts], axis=1)
    return out


def band_allreduce(flat):
    count = lax.axis_size("band")
    radices = []
    rest = count
    while rest % 2 == 0:
        radices.append(2)
        rest //= 2
    if rest != 1:
        return lax.psum(flat, "band")
    length = flat.shape[0]
    flat = jnp.pad(flat, (0, (-length) % count))
    me = lax.axis_index("band")
    steps = []
    stride = 1
    for radix in radices:
        steps.append((stride, radix))
        stride *= radix

    def rotate(stride, radix, u):
        return [
            (j, j + (((j // stride) % radix + u) % radix - (j // stride) % radix) * stride)
            for j in range(count)
        ]

    for stride, radix in steps:
        digit = (me // stride) % radix
        size = flat.shape[0] // radix
        acc = lax.dynamic_slice_in_dim(flat, digit * size, size)
        for u in range(1, radix):
            give = lax.dynamic_slice_in_dim(flat, ((digit + u) % radix) * size, size)
            acc = acc + lax.ppermute(give, "band", rotate(stride, radix, u))
        flat = acc
    for stride, radix in reversed(steps):
        digit = (me // stride) % radix
        size = flat.shape[0]
        full = lax.dynamic_update_slice_in_dim(
            jnp.zeros((size * radix,), flat.dtype), flat, digit * size, 0
        )
        for u in range(1, radix):
            got = lax.ppermute(flat, "band", rotate(stride, radix, u))
            full = lax.dynamic_update_slice_in_dim(full, got, ((digit - u) % radix) * size, 0)
        flat = full
    return flat[:length]


def chan_shift(block, s):
    count = lax.axis_size("chan")
    return lax.ppermute(block, "chan", [(j, (j + s) % count) for j in range(count)])


def block(features, depth_kernel, pointwise, cotangent):
    kernel = depth_kernel.astype(jnp.float32)
    count = lax.axis_size("chan")
    width = pointwise.shape[2] // count
    cot_full = jnp.concatenate(
        [cotangent] + [chan_shift(cotangent, s) for s in range(1, count)], axis=0
    )
    requests = {}
    for spacing in dilations:
        for side in (-1, 1):
            requests[side * spacing] = (features, side * spacing)
    feat_halo = halo_rows(requests)
    me = lax.axis_index("chan")
    pw_slots = [
        lax.dynamic_slice_in_dim(pointwise, ((me - s) % count) * width, width, axis=2)
        for s in range(count)
    ]
    grad_sum = sum(
        jnp.einsum(
            "bco,ohw->bchw", pw_slots[s], cot_full[s * width : (s + 1) * width],
            preferred_element_type=jnp.float32,
        )
        for s in range(count)
    )
    grad_branches = grad_sum.astype(jnp.bfloat16)
    requests = {}
    for which, spacing in enumerate(dilations):
        for side in (-1, 1):
            requests[(which, side * spacing)] = (grad_branches[which + 1], side * spacing)
    grad_halo = halo_rows(requests)

    feat_rows = {0: features.astype(jnp.float32)}
    for offset, rows in feat_halo.items():
        feat_rows[offset] = rows.astype(jnp.float32)
    branches = [features]
    for which, spacing in enumerate(dilations):
        total = jnp.zeros(features.shape, jnp.float32)
        for tap_index in range(9):
            row_step = tap_index // 3 - 1
            col_step = tap_index % 3 - 1
            total = total + kernel[which, tap_index][:, None, None] * jnp.roll(
                feat_rows[row_step * spacing], -col_step * spacing, axis=-1
            )
        branches.append(total.astype(jnp.bfloat16))
    stacked = jnp.stack(branches)

    partial = jnp.einsum(
        "bchw,bco->ohw", stacked, pointwise, preferred_element_type=jnp.float32
    ).astype(jnp.bfloat16)
    result = lax.dynamic_slice_in_dim(partial, me * width, width, axis=0).astype(jnp.float32)
    for s in range(1, count):
        piece = lax.dynamic_slice_in_dim(partial, ((me + s) % count) * width, width, axis=0)
        result = result + chan_shift(piece, s).astype(jnp.float32)
    output = result.astype(jnp.bfloat16)

    point_local = jnp.zeros(pointwise.shape, jnp.float32)
    for s in range(count):
        point_slot = jnp.einsum(
            "bchw,ohw->bco", stacked, cot_full[s * width : (s + 1) * width],
            preferred_element_type=jnp.float32,
        )
        point_local = lax.dynamic_update_slice_in_dim(
            point_local, point_slot, ((me - s) % count) * width, axis=2
        )

    depth_rows = []
    for which, spacing in enumerate(dilations):
        grad_f = grad_branches[which + 1].astype(jnp.float32)
        tap_rows = []
        for tap_index in range(9):
            row_step = tap_index // 3 - 1
            col_step = tap_index % 3 - 1
            tap_rows.append(
                jnp.sum(
                    grad_f * jnp.roll(feat_rows[row_step * spacing], -col_step * spacing, axis=-1),
                    axis=(1, 2),
                )
            )
        depth_rows.append(jnp.stack(tap_rows))
    depth_local = jnp.stack(depth_rows)
    flat = jnp.concatenate([depth_local.reshape(-1), point_local.reshape(-1)])
    flat = band_allreduce(flat)
    depth_total = flat[: depth_local.size].reshape(depth_local.shape)
    point_total = flat[depth_local.size :].reshape(point_local.shape)

    grad_input = grad_branches[0].astype(jnp.float32)
    for which, spacing in enumerate(dilations):
        grad_f = grad_branches[which + 1].astype(jnp.float32)
        for col_step in (-1, 0, 1):
            grad_input = grad_input + kernel[which, 4 + col_step][:, None, None] * jnp.roll(
                grad_f, col_step * spacing, axis=-1
            )
    for which, spacing in enumerate(dilations):
        grad_input = lax.optimization_barrier(grad_input)
        for row_step in (-1, 1):
            rows = grad_halo[(which, -row_step * spacing)].astype(jnp.float32)
            for col_step in (-1, 0, 1):
                tap_index = (row_step + 1) * 3 + col_step + 1
                grad_input = grad_input + kernel[which, tap_index][:, None, None] * jnp.roll(
                    rows, col_step * spacing, axis=-1
                )
    return (output, grad_input, depth_total / GSCALE, point_total / GSCALE)


def solution(mesh):
    return jax.shard_map(
        block,
        mesh=mesh,
        in_specs=(
            P("chan", "band", None),
            P(None, None, "chan"),
            P(None, "chan", None),
            P("chan", "band", None),
        ),
        out_specs=(
            P("chan", "band", None),
            P("chan", "band", None),
            P(None, None, "chan"),
            P(None, "chan", None),
        ),
        check_vma=False,
    )
```

profile of v0, /device:TPU:3, one launch (start us, length us, event | category | flops | bytes accessed | tf_op | source)
XLA Modules:
  0.0 317.8 jit_solution(13177942275023706523)
XLA Ops:
  4.9 6.6 %collective-permute-start.6 = (bf16[128,2,1024]{0,2,1:T(8,128)(2,1)}, bf16[128,2,1024]{0,2,1:T(8,128)(2,1)}, u32[]{:S(2)}, u32[]{:S(2)}) collective-permute-start(bf16[128,2,1024]{0,2,1:T(8,128)(2,1)} %get-tuple-element.123), channel_id=1, source_target_pairs={{0,10},{2,12},{4,14},{6,16},{8,18},{10,20},{12,22},{14,24},{16,26}... | collective-permute-start | bytes 1572872 | tf_op jit(solution)/shard_map/ppermute | solution.py:18
  13.5 2.3 collective-permute-start
  15.8 4.8 %collective-permute-start.7 = (bf16[128,2,1024]{0,2,1:T(8,128)(2,1)}, bf16[128,2,1024]{0,2,1:T(8,128)(2,1)}, u32[]{:S(2)}, u32[]{:S(2)}) collective-permute-start(bf16[128,2,1024]{0,2,1:T(8,128)(2,1)} %get-tuple-element.124), channel_id=1, source_target_pairs={{0,8},{2,10},{4,12},{6,14},{8,16},{10,18},{12,20},{14,22},{16,24},... | collective-permute-start | bytes 1572872 | tf_op jit(solution)/shard_map/ppermute | solution.py:18
  21.9 2.2 fusion.132
  24.1 2.2 fusion.128
  29.4 2.6 copy.33
  31.9 2.5 fusion.78
  35.8 8.3 %collective-permute-done.7 = bf16[128,2,1024]{0,2,1:T(8,128)(2,1)} collective-permute-done((bf16[128,2,1024]{0,2,1:T(8,128)(2,1)}, bf16[128,2,1024]{0,2,1:T(8,128)(2,1)}, u32[]{:S(2)}, u32[]{:S(2)}) %collective-permute-start.7) | collective-permute-done | bytes 524320 | tf_op jit(solution)/shard_map/ppermute | solution.py:18
  47.3 2.2 fusion.114
  49.5 3.6 %collective-permute-start.1 = (bf16[128,2,1024]{0,2,1:T(8,128)(2,1)}, bf16[128,2,1024]{0,2,1:T(8,128)(2,1)S(1)}, u32[]{:S(2)}, u32[]{:S(2)}) collective-permute-start(bf16[128,2,1024]{0,2,1:T(8,128)(2,1)} %get-tuple-element.124), channel_id=1, source_target_pairs={{0,2},{2,4},{4,6},{6,8},{8,10},{10,12},{12,14},{14,16},{16,18},{18... | collective-permute-start | bytes 1572872 | tf_op jit(solution)/shard_map/ppermute | solution.py:18
  53.1 4.6 %collective-permute-done.9 = bf16[128,2,1024]{0,2,1:T(8,128)(2,1)S(1)} collective-permute-done((bf16[128,2,1024]{0,2,1:T(8,128)(2,1)}, bf16[128,2,1024]{0,2,1:T(8,128)(2,1)S(1)}, u32[]{:S(2)}, u32[]{:S(2)}) %collective-permute-start.9) | collective-permute-done | bytes 524320 | tf_op jit(solution)/shard_map/ppermute | solution.py:18
  61.2 3.9 %collective-permute-start.4 = (bf16[128,4,1024]{0,2,1:T(8,128)(2,1)S(1)}, bf16[128,4,1024]{0,2,1:T(8,128)(2,1)S(1)}, u32[]{:S(2)}, u32[]{:S(2)}) collective-permute-start(bf16[128,4,1024]{0,2,1:T(8,128)(2,1)S(1)} %copy.25), channel_id=1, source_target_pairs={{0,6},{2,8},{4,10},{6,12},{8,14},{10,16},{12,18},{14,20},{16,22},{... | collective-permute-start | bytes 3145736 | tf_op jit(solution)/shard_map/ppermute | solution.py:18
  68.1 2.2 maximum_convert_fusion
  70.8 6.1 %fusion.80 = bf16[1,128,4,1024]{1,3,0,2:T(8,128)(2,1)} fusion(f32[128,4,18]{0,2,1:T(8,128)S(1)} %get-tuple-element.88, f32[128,4,1006]{0,2,1:T(8,128)S(1)} %get-tuple-element.90, f32[128]{0:T(128)S(1)} %copy-done.74, f32[128]{0:T(128)S(1)} %copy-done.76, f32[128,4,1006]{0,2,1:T(8,128)S(1)} %get-tuple-element.89, f32[128,4,18]{0,2,1:T(8,128)S(1)} %get-tuple-element.87, ...), kind=kLoop, calls=%fused_computation.168 | loop fusion | flops 15204352 | bytes 16781824 | tf_op jit(solution)/shard_map/stack | solution.py:144
  78.6 5.6 %fusion.82 = bf16[1,128,4,1024]{1,3,0,2:T(8,128)(2,1)} fusion(f32[128,4,6]{0,2,1:T(8,128)S(1)} %get-tuple-element.80, f32[128,4,1018]{0,2,1:T(8,128)S(1)} %get-tuple-element.82, f32[128]{0:T(128)S(1)} %copy-done.102, f32[128]{0:T(128)S(1)} %copy-done.104, f32[128,4,1018]{0,2,1:T(8,128)S(1)} %get-tuple-element.81, f32[128,4,6]{0,2,1:T(8,128)S(1)} %get-tuple-element.79, ...), kind=kLoop, calls=%fused_computation.170 | loop fusion | flops 15204352 | bytes 16781824 | tf_op jit(solution)/shard_map/stack | solution.py:144
  84.2 5.9 %collective-permute-done.11 = bf16[128,4,1024]{2,0,1:T(8,128)(2,1)} collective-permute-done((bf16[128,4,1024]{2,0,1:T(8,128)(2,1)}, bf16[128,4,1024]{2,0,1:T(8,128)(2,1)}, u32[]{:S(2)}, u32[]{:S(2)}) %collective-permute-start.11) | collective-permute-done | bytes 1048608 | tf_op jit(solution)/shard_map/ppermute | solution.py:97
  90.1 2.5 add_convert_fusion
  92.7 3.5 %slice_bitcast_fusion = (bf16[128,4,1024]{0,2,1:T(8,128)(2,1)}, f32[128,4,1024]{0,2,1:T(8,128)}, f32[128,4,1024]{0,2,1:T(8,128)S(1)}, f32[128,4,1024]{0,2,1:T(8,...) fusion(bf16[4,128,4,1024]{1,3,2,0:T(8,128)(2,1)S(1)} %add_convert_fusion), kind=kLoop, calls=%fused_computation.150 | loop fusion | flops 1572864 | bytes 12582912 | tf_op jit(solution)/shard_map/squeeze | solution.py:187
  97.1 2.3 fusion.108
  102.5 2.4 fusion.32
  105.0 4.9 %fusion.81 = bf16[1,128,4,1024]{1,3,0,2:T(8,128)(2,1)} fusion(f32[128,4,12]{0,2,1:T(8,128)S(1)} %get-tuple-element.116, f32[128,4,1012]{0,2,1:T(8,128)S(1)} %get-tuple-element.118, f32[128]{0:T(128)S(1)} %copy-done.86, bf16[128,4,1024]{0,2,1:T(8,128)(2,1)S(1)} %collective-permute-done.5, f32[128]{0:T(128)S(1)} %copy-done.88, f32[128,4,1012]{0,2,1:T(8,128)} %copy-done.11, ...), kind=kLoop, calls=%fused_computation.169 | loop fusion | flops 14155776 | bytes 16781824 | tf_op jit(solution)/shard_map/stack | solution.py:144
  109.9 3.0 fusion.74
  113.0 2.7 fusion.73
  116.7 4.8 %fusion.30 = (f32[128]{0:T(128)}, f32[128]{0:T(128)}, f32[128]{0:T(128)}, f32[128]{0:T(128)}, f32[128]{0:T(128)}, /*index=5*/f32[128]{0:T(128)}, f32[128]{0:T(128)}, f32[128]{0:T(128)}) fusion(bf16[128,4,1024]{0,2,1:T(8,128)(2,1)S(1)} %copy.25, bf16[4,128,4,1024]{1,3,2,0:T(8,128)(2,1)S(1)} %add_convert_fusion, f32[128,4,6]{0,2,1:T(8,128)S(1)} %copy-done.45, ...), kind=kLoop, calls=%fused_computation.66 | loop fusion | flops 13630464 | bytes 13635584 | tf_op jit(solution)/shard_map/reduce_sum | solution.py:173
  121.5 4.5 %fusion.33 = (f32[128]{0:T(128)}, f32[128]{0:T(128)}, f32[128]{0:T(128)}, f32[128]{0:T(128)}, f32[128]{0:T(128)}, /*index=5*/f32[128]{0:T(128)}, f32[128]{0:T(128)}) fusion(bf16[128,2,1024]{0,2,1:T(8,128)(2,1)S(1)} %collective-permute-done.3, bf16[128,2,1024]{0,2,1:T(8,128)(2,1)} %collective-permute-done.2, ...), kind=kLoop, calls=%fused_computation.69 | loop fusion | flops 13630592 | bytes 13635072 | tf_op jit(solution)/shard_map/reduce_sum | solution.py:173
  126.0 2.5 stack.142
  128.5 7.1 %fusion.34 = (f32[128]{0:T(128)}, f32[128]{0:T(128)}, f32[128]{0:T(128)}, f32[128]{0:T(128)}, f32[128]{0:T(128)}, /*index=5*/f32[128]{0:T(128)}) fusion(f32[128,4,6]{0,2,1:T(8,128)} %copy-done.46, f32[128,4,1018]{0,2,1:T(8,128)} %copy-done.8, bf16[4,128,4,1024]{1,3,2,0:T(8,128)(2,1)} %copy-done.1, f32[128,4,18]{0,2,1:T(8,128)} %copy-done.40, ...), kind=kLoop, calls=%fused_computation.70 | loop fusion | flops 11009280 | bytes 13634560 | tf_op jit(solution)/shard_map/reduce_sum | solution.py:173
  143.5 9.0 %collective-permute-start.22 = (f32[67264]{0:T(1024)S(1)}, f32[67264]{0:T(1024)S(1)}, u32[]{:S(2)}, u32[]{:S(2)}) collective-permute-start(f32[67264]{0:T(1024)S(1)} %dynamic_slice.41), channel_id=1, source_target_pairs={{0,2},{2,0},{4,6},{6,4},{8,10},{10,8},{12,14},{14,12},{16,18},{18,... | collective-permute-start | bytes 807176 | tf_op jit(solution)/shard_map/ppermute | solution.py:80
  152.5 2.2 fusion.117
  156.2 8.8 %collective-permute-start.15 = (bf16[128,2,1024]{0,2,1:T(8,128)(2,1)S(1)}, bf16[128,2,1024]{0,2,1:T(8,128)(2,1)S(1)}, u32[]{:S(2)}, u32[]{:S(2)}) collective-permute-start(bf16[128,2,1024]{0,2,1:T(8,128)(2,1)S(1)} %get-tuple-element.102), channel_id=1, source_target_pairs={{0,2},{2,4},{4,6},{6,8},{8,10},{10,12},{12,14},{14,16},{16,18},{18... | collective-permute-start | bytes 1572872 | tf_op jit(solution)/shard_map/ppermute | solution.py:18
  170.1 4.2 %fusion.25 = f32[128,4,1024]{0,2,1:T(8,128)S(1)} fusion(f32[128,4,6]{0,2,1:T(8,128)S(1)} %copy-done.54, f32[128,4,1018]{0,2,1:T(8,128)S(1)} %copy-done.19, f32[128,4,1018]{0,2,1:T(8,128)S(1)} %copy-done.18, f32[128,4,6]{0,2,1:T(8,128)S(1)} %copy-done.53, f32[128,4,12]{0,2,1:T(8,128)S(1)} %get-tuple-element.68, f32[128,4,1012]{0,2,1:T(8,128)S(1)} %get-tuple-element.70, ...), kind=kLoop, calls=%fused_computation.61 | loop fusion | flops 14680064 | bytes 18878976 | tf_op jit(solution)/shard_map/add | solution.py:189
  174.5 2.8 collective-permute-start.24
  178.9 5.4 %collective-permute-start.20 = (bf16[128,2,1024]{0,2,1:T(8,128)(2,1)}, bf16[128,2,1024]{0,2,1:T(8,128)(2,1)}, u32[]{:S(2)}, u32[]{:S(2)}) collective-permute-start(bf16[128,2,1024]{0,2,1:T(8,128)(2,1)} %get-tuple-element.91), channel_id=1, source_target_pairs={{0,10},{2,12},{4,14},{6,16},{8,18},{10,20},{12,22},{14,24},{16,26}... | collective-permute-start | bytes 1572872 | tf_op jit(solution)/shard_map/ppermute | solution.py:18
  187.5 17.8 %collective-permute-done.25 = f32[8408]{0:T(1024)S(1)} collective-permute-done((f32[8408]{0:T(1024)S(1)}, f32[8408]{0:T(1024)S(1)}, u32[]{:S(2)}, u32[]{:S(2)}) %collective-permute-start.25) | collective-permute-done | bytes 33664 | tf_op jit(solution)/shard_map/ppermute | solution.py:80
  209.6 10.6 %collective-permute-start.21 = (bf16[128,2,1024]{0,2,1:T(8,128)(2,1)}, bf16[128,2,1024]{0,2,1:T(8,128)(2,1)}, u32[]{:S(2)}, u32[]{:S(2)}) collective-permute-start(bf16[128,2,1024]{0,2,1:T(8,128)(2,1)} %get-tuple-element.92), channel_id=1, source_target_pairs={{0,8},{2,10},{4,12},{6,14},{8,16},{10,18},{12,20},{14,22},{16,24},... | collective-permute-start | bytes 1572872 | tf_op jit(solution)/shard_map/ppermute | solution.py:18
  221.9 2.4 collective-permute-done.13
  224.4 3.2 collective-permute-start.16
  228.4 3.5 %fusion.59 = f32[128,4,1024]{0,2,1:T(8,128)} fusion(f32[128,4,1024]{0,2,1:T(8,128)S(1)} %fusion.25, f32[128,4,6]{0,2,1:T(8,128)S(1)} %get-tuple-element.60, f32[128,4,1018]{0,2,1:T(8,128)S(1)} %get-tuple-element.62, f32[128,4,1018]{0,2,1:T(8,128)S(1)} %get-tuple-element.61, f32[128,4,6]{0,2,1:T(8,128)S(1)} %get-tuple-element.59, ...), kind=kLoop, calls=%fused_computation.120 | loop fusion | flops 10485760 | bytes 14683136 | tf_op jit(solution)/shard_map/add | solution.py:198
  231.9 21.0 %collective-permute-start.17 = (bf16[128,4,1024]{0,2,1:T(8,128)(2,1)}, bf16[128,4,1024]{0,2,1:T(8,128)(2,1)S(1)}, u32[]{:S(2)}, u32[]{:S(2)}) collective-permute-start(bf16[128,4,1024]{0,2,1:T(8,128)(2,1)} %get-tuple-element.45), channel_id=1, source_target_pairs={{0,6},{2,8},{4,10},{6,12},{8,14},{10,16},{12,18},{14,20},{16,22},{... | collective-permute-start | bytes 3145736 | tf_op jit(solution)/shard_map/ppermute | solution.py:18
  252.9 2.2 collective-permute-done.19
  255.3 2.5 fusion.98
  258.0 7.2 %collective-permute-done.26 = f32[8408]{0:T(1024)S(1)} collective-permute-done((f32[8408]{0:T(1024)S(1)}, f32[8408]{0:T(1024)S(1)}, u32[]{:S(2)}, u32[]{:S(2)}) %collective-permute-start.26) | collective-permute-done | bytes 33664 | tf_op jit(solution)/shard_map/ppermute | solution.py:89
  267.2 2.7 maximum_convert_fusion.7
  271.4 9.0 %collective-permute-start.28 = (f32[33632]{0:T(1024)S(1)}, f32[33632]{0:T(1024)S(1)}, u32[]{:S(2)}, u32[]{:S(2)}) collective-permute-start(f32[33632]{0:T(1024)S(1)} %dynamic_update_slice.35), channel_id=1, source_target_pairs={{0,4},{2,6},{4,0},{6,2},{8,12},{10,14},{12,8},{14,10},{16,20},{18,... | collective-permute-start | bytes 403592 | tf_op jit(solution)/shard_map/ppermute | solution.py:89
  280.4 4.4 %fusion.96 = (f32[128,4,1006]{0,2,1:T(8,128)}, f32[128,4,1006]{0,2,1:T(8,128)}) fusion(f32[128,4,1024]{0,2,1:T(8,128)} %maximum_convert_fusion.7), kind=kLoop, calls=%fused_computation.220 | loop fusion | bytes 8241152 | tf_op jit(solution)/shard_map/jit(_roll_static)/slice | solution.py:198
  287.1 4.7 %collective-permute-start.29 = (f32[67264]{0:T(1024)S(1)}, f32[67264]{0:T(1024)}, u32[]{:S(2)}, u32[]{:S(2)}) collective-permute-start(f32[67264]{0:T(1024)S(1)} %dynamic_update_slice.37), channel_id=1, source_target_pairs={{0,2},{2,0},{4,6},{6,4},{8,10},{10,8},{12,14},{14,12},{16,18},{18,... | collective-permute-start | bytes 807176 | tf_op jit(solution)/shard_map/ppermute | solution.py:89
  296.1 3.4 %dynamic_update_slice.39 = f32[134528]{0:T(1024)S(1)} dynamic-update-slice(f32[134528]{0:T(1024)S(1)} %dynamic_update_slice.38, f32[67264]{0:T(1024)} %collective-permute-done.29, s32[]{:T(128)S(6)} %select_n.177) | dynamic-update-slice | bytes 538116 | tf_op jit(solution)/shard_map/dynamic_update_slice | solution.py:90
  312.0 3.6 %fusion.71 = f32[128,4,1024]{0,2,1:T(8,128)S(1)} fusion(f32[128,4,1024]{0,2,1:T(8,128)S(1)} %fusion.65, f32[128,4,18]{0,2,1:T(8,128)S(1)} %get-tuple-element.52, f32[128,4,1006]{0,2,1:T(8,128)S(1)} %copy-done.22, f32[128,4,1006]{0,2,1:T(8,128)S(1)} %copy-done.21, f32[128,4,18]{0,2,1:T(8,128)S(1)} %get-tuple-element.51, f32[128,4,18]{0,2,1:T(8,128)S(1)} %copy-done.43, ...), kind=kLoop, calls=%fused_computation.140 | loop fusion | flops 10485760 | bytes 14683136 | tf_op jit(solution)/shard_map/add | solution.py:198
  (339 shorter events, 78.8 us)
Async XLA Ops:
  0.6 31.3 %copy-start = (bf16[4,128,256]{2,1,0:T(8,128)(2,1)S(1)}, bf16[4,128,256]{2,1,0:T(8,128)(2,1)}, u32[]{:S(2)}) copy-start(bf16[4,128,256]{2,1,0:T(8,128)(2,1)} %param.6) | copy-start | bytes 786436
  3.7 45.9 %collective-permute-start.8 = (bf16[128,2,1024]{0,2,1:T(8,128)(2,1)}, bf16[128,2,1024]{0,2,1:T(8,128)(2,1)}, u32[]{:S(2)}, u32[]{:S(2)}) collective-permute-start(bf16[128,2,1024]{0,2,1:T(8,128)(2,1)} %get-tuple-element.123), channel_id=1, source_target_pairs={{8,0},{10,2},{12,4},{14,6},{16,8},{18,10},{20,12},{22,14},{24,16},... | collective-permute-start | bytes 1572872 | tf_op jit(solution)/shard_map/ppermute | solution.py:18
  4.9 29.5 %collective-permute-start.6 = (bf16[128,2,1024]{0,2,1:T(8,128)(2,1)}, bf16[128,2,1024]{0,2,1:T(8,128)(2,1)}, u32[]{:S(2)}, u32[]{:S(2)}) collective-permute-start(bf16[128,2,1024]{0,2,1:T(8,128)(2,1)} %get-tuple-element.123), channel_id=1, source_target_pairs={{0,10},{2,12},{4,14},{6,16},{8,18},{10,20},{12,22},{14,24},{16,26}... | collective-permute-start | bytes 1572872 | tf_op jit(solution)/shard_map/ppermute | solution.py:18
  11.6 49.6 %collective-permute-start.2 = (bf16[128,2,1024]{0,2,1:T(8,128)(2,1)}, bf16[128,2,1024]{0,2,1:T(8,128)(2,1)}, u32[]{:S(2)}, u32[]{:S(2)}) collective-permute-start(bf16[128,2,1024]{0,2,1:T(8,128)(2,1)} %get-tuple-element.123), channel_id=1, source_target_pairs={{2,0},{4,2},{6,4},{8,6},{10,8},{12,10},{14,12},{16,14},{18,16},{20... | collective-permute-start | bytes 1572872 | tf_op jit(solution)/shard_map/ppermute | solution.py:18
  13.5 54.6 %collective-permute-start = (bf16[128,2,1024]{0,2,1:T(8,128)(2,1)}, bf16[128,2,1024]{0,2,1:T(8,128)(2,1)}, u32[]{:S(2)}, u32[]{:S(2)}) collective-permute-start(bf16[128,2,1024]{0,2,1:T(8,128)(2,1)} %get-tuple-element.123), channel_id=1, source_target_pairs={{0,4},{2,6},{4,8},{6,10},{8,12},{10,14},{12,16},{14,18},{16,20},{1... | collective-permute-start | bytes 1572872 | tf_op jit(solution)/shard_map/ppermute | solution.py:18
  15.8 28.2 %collective-permute-start.7 = (bf16[128,2,1024]{0,2,1:T(8,128)(2,1)}, bf16[128,2,1024]{0,2,1:T(8,128)(2,1)}, u32[]{:S(2)}, u32[]{:S(2)}) collective-permute-start(bf16[128,2,1024]{0,2,1:T(8,128)(2,1)} %get-tuple-element.124), channel_id=1, source_target_pairs={{0,8},{2,10},{4,12},{6,14},{8,16},{10,18},{12,20},{14,22},{16,24},... | collective-permute-start | bytes 1572872 | tf_op jit(solution)/shard_map/ppermute | solution.py:18
  27.9 49.5 %copy-start.5 = (f32[128,4,1018]{0,2,1:T(8,128)}, f32[128,4,1018]{0,2,1:T(8,128)S(1)}, u32[]{:S(2)}) copy-start(f32[128,4,1018]{0,2,1:T(8,128)S(1)} %get-tuple-element.105) | copy-start | bytes 6254596
  34.5 23.3 %collective-permute-start.9 = (bf16[128,2,1024]{0,2,1:T(8,128)(2,1)}, bf16[128,2,1024]{0,2,1:T(8,128)(2,1)S(1)}, u32[]{:S(2)}, u32[]{:S(2)}) collective-permute-start(bf16[128,2,1024]{0,2,1:T(8,128)(2,1)} %get-tuple-element.124), channel_id=1, source_target_pairs={{10,0},{12,2},{14,4},{16,6},{18,8},{20,10},{22,12},{24,14},{26,16}... | collective-permute-start | bytes 1572872 | tf_op jit(solution)/shard_map/ppermute | solution.py:18
  44.0 21.1 %collective-permute-start.3 = (bf16[128,2,1024]{0,2,1:T(8,128)(2,1)}, bf16[128,2,1024]{0,2,1:T(8,128)(2,1)S(1)}, u32[]{:S(2)}, u32[]{:S(2)}) collective-permute-start(bf16[128,2,1024]{0,2,1:T(8,128)(2,1)} %get-tuple-element.124), channel_id=1, source_target_pairs={{4,0},{6,2},{8,4},{10,6},{12,8},{14,10},{16,12},{18,14},{20,16},{2... | collective-permute-start | bytes 1572872 | tf_op jit(solution)/shard_map/ppermute | solution.py:18
  49.5 18.6 %collective-permute-start.1 = (bf16[128,2,1024]{0,2,1:T(8,128)(2,1)}, bf16[128,2,1024]{0,2,1:T(8,128)(2,1)S(1)}, u32[]{:S(2)}, u32[]{:S(2)}) collective-permute-start(bf16[128,2,1024]{0,2,1:T(8,128)(2,1)} %get-tuple-element.124), channel_id=1, source_target_pairs={{0,2},{2,4},{4,6},{6,8},{8,10},{10,12},{12,14},{14,16},{16,18},{18... | collective-permute-start | bytes 1572872 | tf_op jit(solution)/shard_map/ppermute | solution.py:18
  57.7 12.6 %copy-start.25 = (bf16[128,2,1024]{0,2,1:T(8,128)(2,1)}, bf16[128,2,1024]{0,2,1:T(8,128)(2,1)S(1)}, u32[]{:S(2)}) copy-start(bf16[128,2,1024]{0,2,1:T(8,128)(2,1)S(1)} %collective-permute-done.9) | copy-start | bytes 1572868
  57.7 41.6 %collective-permute-start.5 = (bf16[128,4,1024]{0,2,1:T(8,128)(2,1)S(1)}, bf16[128,4,1024]{0,2,1:T(8,128)(2,1)S(1)}, u32[]{:S(2)}, u32[]{:S(2)}) collective-permute-start(bf16[128,4,1024]{0,2,1:T(8,128)(2,1)S(1)} %copy.25), channel_id=1, source_target_pairs={{6,0},{8,2},{10,4},{12,6},{14,8},{16,10},{18,12},{20,14},{22,16},{... | collective-permute-start | bytes 3145736 | tf_op jit(solution)/shard_map/ppermute | solution.py:18
  60.9 9.5 %copy-start.40 = (f32[128,4,18]{0,2,1:T(8,128)}, f32[128,4,18]{0,2,1:T(8,128)S(1)}, u32[]{:S(2)}) copy-start(f32[128,4,18]{0,2,1:T(8,128)S(1)} %get-tuple-element.88) | copy-start | bytes 110596
  61.2 9.2 %copy-start.14 = (f32[128,4,1006]{0,2,1:T(8,128)}, f32[128,4,1006]{0,2,1:T(8,128)S(1)}, u32[]{:S(2)}) copy-start(f32[128,4,1006]{0,2,1:T(8,128)S(1)} %get-tuple-element.89) | copy-start | bytes 6180868
  61.2 9.2 %copy-start.15 = (f32[128,4,1006]{0,2,1:T(8,128)}, f32[128,4,1006]{0,2,1:T(8,128)S(1)}, u32[]{:S(2)}) copy-start(f32[128,4,1006]{0,2,1:T(8,128)S(1)} %get-tuple-element.90) | copy-start | bytes 6180868
  61.2 35.6 %collective-permute-start.4 = (bf16[128,4,1024]{0,2,1:T(8,128)(2,1)S(1)}, bf16[128,4,1024]{0,2,1:T(8,128)(2,1)S(1)}, u32[]{:S(2)}, u32[]{:S(2)}) collective-permute-start(bf16[128,4,1024]{0,2,1:T(8,128)(2,1)S(1)} %copy.25), channel_id=1, source_target_pairs={{0,6},{2,8},{4,10},{6,12},{8,14},{10,16},{12,18},{14,20},{16,22},{... | collective-permute-start | bytes 3145736 | tf_op jit(solution)/shard_map/ppermute | solution.py:18
  65.1 25.0 %collective-permute-start.11 = (bf16[128,4,1024]{2,0,1:T(8,128)(2,1)}, bf16[128,4,1024]{2,0,1:T(8,128)(2,1)}, u32[]{:S(2)}, u32[]{:S(2)}) collective-permute-start(bf16[128,4,1024]{2,0,1:T(8,128)(2,1)} %copy.33), channel_id=1, source_target_pairs={{0,1},{1,0},{2,3},{3,2},{4,5},{5,4},{6,7},{7,6},{8,9},{9,8},{10,11... | collective-permute-start | bytes 3145736 | tf_op jit(solution)/shard_map/ppermute | solution.py:97
  67.6 9.7 %copy-start.46 = (f32[128,4,6]{0,2,1:T(8,128)}, f32[128,4,6]{0,2,1:T(8,128)S(1)}, u32[]{:S(2)}) copy-start(f32[128,4,6]{0,2,1:T(8,128)S(1)} %get-tuple-element.80) | copy-start | bytes 36868
  67.7 9.7 %copy-start.51 = (f32[128,4,6]{0,2,1:T(8,128)}, f32[128,4,6]{0,2,1:T(8,128)S(1)}, u32[]{:S(2)}) copy-start(f32[128,4,6]{0,2,1:T(8,128)S(1)} %get-tuple-element.79) | copy-start | bytes 36868
  68.0 9.4 %copy-start.8 = (f32[128,4,1018]{0,2,1:T(8,128)}, f32[128,4,1018]{0,2,1:T(8,128)S(1)}, u32[]{:S(2)}) copy-start(f32[128,4,1018]{0,2,1:T(8,128)S(1)} %get-tuple-element.82) | copy-start | bytes 6254596
  70.3 7.1 %copy-start.47 = (f32[128,4,6]{0,2,1:T(8,128)}, f32[128,4,6]{0,2,1:T(8,128)S(1)}, u32[]{:S(2)}) copy-start(f32[128,4,6]{0,2,1:T(8,128)S(1)} %get-tuple-element.75) | copy-start | bytes 36868
  70.3 7.1 %copy-start.49 = (f32[128,4,6]{0,2,1:T(8,128)}, f32[128,4,6]{0,2,1:T(8,128)S(1)}, u32[]{:S(2)}) copy-start(f32[128,4,6]{0,2,1:T(8,128)S(1)} %get-tuple-element.76) | copy-start | bytes 36868
  92.7 28.8 %copy-start.1 = (bf16[4,128,4,1024]{1,3,2,0:T(8,128)(2,1)}, bf16[4,128,4,1024]{1,3,2,0:T(8,128)(2,1)S(1)}, u32[]{:S(2)}) copy-start(bf16[4,128,4,1024]{1,3,2,0:T(8,128)(2,1)S(1)} %add_convert_fusion) | copy-start | bytes 12582916
  139.0 17.1 %copy-start.27 = (bf16[128,4,1024]{0,2,1:T(8,128)(2,1)S(1)}, bf16[128,4,1024]{0,2,1:T(8,128)(2,1)}, u32[]{:S(2)}) copy-start(bf16[128,4,1024]{0,2,1:T(8,128)(2,1)} %get-tuple-element.46) | copy-start | bytes 3145732
  143.5 23.4 %collective-permute-start.22 = (f32[67264]{0:T(1024)S(1)}, f32[67264]{0:T(1024)S(1)}, u32[]{:S(2)}, u32[]{:S(2)}) collective-permute-start(f32[67264]{0:T(1024)S(1)} %dynamic_slice.41), channel_id=1, source_target_pairs={{0,2},{2,0},{4,6},{6,4},{8,10},{10,8},{12,14},{14,12},{16,18},{18,... | collective-permute-start | bytes 807176 | tf_op jit(solution)/shard_map/ppermute | solution.py:80
  154.8 77.1 %collective-permute-start.18 = (bf16[128,2,1024]{0,2,1:T(8,128)(2,1)}, bf16[128,2,1024]{0,2,1:T(8,128)(2,1)S(1)}, u32[]{:S(2)}, u32[]{:S(2)}) collective-permute-start(bf16[128,2,1024]{0,2,1:T(8,128)(2,1)} %get-tuple-element.91), channel_id=1, source_target_pairs={{8,0},{10,2},{12,4},{14,6},{16,8},{18,10},{20,12},{22,14},{24,16},... | collective-permute-start | bytes 1572872 | tf_op jit(solution)/shard_map/ppermute | solution.py:18
  156.2 53.4 %collective-permute-start.15 = (bf16[128,2,1024]{0,2,1:T(8,128)(2,1)S(1)}, bf16[128,2,1024]{0,2,1:T(8,128)(2,1)S(1)}, u32[]{:S(2)}, u32[]{:S(2)}) collective-permute-start(bf16[128,2,1024]{0,2,1:T(8,128)(2,1)S(1)} %get-tuple-element.102), channel_id=1, source_target_pairs={{0,2},{2,4},{4,6},{6,8},{8,10},{10,12},{12,14},{14,16},{16,18},{18... | collective-permute-start | bytes 1572872 | tf_op jit(solution)/shard_map/ppermute | solution.py:18
  167.3 7.0 %collective-permute-start.23 = (f32[33632]{0:T(1024)S(1)}, f32[33632]{0:T(1024)S(1)}, u32[]{:S(2)}, u32[]{:S(2)}) collective-permute-start(f32[33632]{0:T(1024)S(1)} %dynamic_slice.43), channel_id=1, source_target_pairs={{0,4},{2,6},{4,0},{6,2},{8,12},{10,14},{12,8},{14,10},{16,20},{18,... | collective-permute-start | bytes 403592 | tf_op jit(solution)/shard_map/ppermute | solution.py:80
  170.1 7.3 %copy-start.34 = (bf16[1,128,4,1024]{1,3,0,2:T(8,128)(2,1)S(1)}, bf16[1,128,4,1024]{1,3,0,2:T(8,128)(2,1)}, u32[]{:S(2)}) copy-start(bf16[1,128,4,1024]{1,3,0,2:T(8,128)(2,1)} %fusion.80) | copy-start | bytes 3145732
  170.1 7.3 %copy-start.36 = (bf16[1,128,4,1024]{1,3,0,2:T(8,128)(2,1)S(1)}, bf16[1,128,4,1024]{1,3,0,2:T(8,128)(2,1)}, u32[]{:S(2)}) copy-start(bf16[1,128,4,1024]{1,3,0,2:T(8,128)(2,1)} %fusion.82) | copy-start | bytes 3145732
  170.1 7.3 %copy-start.38 = (bf16[1,128,4,1024]{1,3,0,2:T(8,128)(2,1)S(1)}, bf16[1,128,4,1024]{1,3,0,2:T(8,128)(2,1)}, u32[]{:S(2)}) copy-start(bf16[1,128,4,1024]{1,3,0,2:T(8,128)(2,1)} %fusion.81) | copy-start | bytes 3145732
  174.5 11.6 %collective-permute-start.24 = (f32[16816]{0:T(1024)S(1)}, f32[16816]{0:T(1024)S(1)}, u32[]{:S(2)}, u32[]{:S(2)}) collective-permute-start(f32[16816]{0:T(1024)S(1)} %dynamic_slice.45), channel_id=1, source_target_pairs={{0,8},{2,10},{4,12},{6,14},{8,0},{10,2},{12,4},{14,6},{16,24},{18,... | collective-permute-start | bytes 201800 | tf_op jit(solution)/shard_map/ppermute | solution.py:80
  178.9 30.7 %copy-start.28 = (bf16[4,1024,256]{2,1,0:T(8,128)(2,1)}, bf16[4,1024,256]{2,1,0:T(8,128)(2,1)S(1)}, u32[]{:S(2)}) copy-start(bf16[4,1024,256]{2,1,0:T(8,128)(2,1)S(1)} %bitcast_convert_fusion) | copy-start | bytes 6291460
  178.9 88.3 %collective-permute-start.20 = (bf16[128,2,1024]{0,2,1:T(8,128)(2,1)}, bf16[128,2,1024]{0,2,1:T(8,128)(2,1)}, u32[]{:S(2)}, u32[]{:S(2)}) collective-permute-start(bf16[128,2,1024]{0,2,1:T(8,128)(2,1)} %get-tuple-element.91), channel_id=1, source_target_pairs={{0,10},{2,12},{4,14},{6,16},{8,18},{10,20},{12,22},{14,24},{16,26}... | collective-permute-start | bytes 1572872 | tf_op jit(solution)/shard_map/ppermute | solution.py:18
  184.2 23.4 %collective-permute-start.14 = (bf16[128,2,1024]{0,2,1:T(8,128)(2,1)S(1)}, bf16[128,2,1024]{0,2,1:T(8,128)(2,1)S(1)}, u32[]{:S(2)}, u32[]{:S(2)}) collective-permute-start(bf16[128,2,1024]{0,2,1:T(8,128)(2,1)S(1)} %get-tuple-element.101), channel_id=1, source_target_pairs={{0,4},{2,6},{4,8},{6,10},{8,12},{10,14},{12,16},{14,18},{16,20},{1... | collective-permute-start | bytes 1572872 | tf_op jit(solution)/shard_map/ppermute | solution.py:18
  186.3 19.0 %collective-permute-start.25 = (f32[8408]{0:T(1024)S(1)}, f32[8408]{0:T(1024)S(1)}, u32[]{:S(2)}, u32[]{:S(2)}) collective-permute-start(f32[8408]{0:T(1024)S(1)} %dynamic_slice.47), channel_id=1, source_target_pairs={{0,16},{2,18},{4,20},{6,22},{8,24},{10,26},{12,28},{14,30},{16,0},... | collective-permute-start | bytes 100904 | tf_op jit(solution)/shard_map/ppermute | solution.py:80
  205.4 15.3 %collective-permute-start.12 = (bf16[128,2,1024]{0,2,1:T(8,128)(2,1)S(1)}, bf16[128,2,1024]{0,2,1:T(8,128)(2,1)S(1)}, u32[]{:S(2)}, u32[]{:S(2)}) collective-permute-start(bf16[128,2,1024]{0,2,1:T(8,128)(2,1)S(1)} %get-tuple-element.101), channel_id=1, source_target_pairs={{2,0},{4,2},{6,4},{8,6},{10,8},{12,10},{14,12},{16,14},{18,16},{20... | collective-permute-start | bytes 1572872 | tf_op jit(solution)/shard_map/ppermute | solution.py:18
  207.6 16.7 %collective-permute-start.13 = (bf16[128,2,1024]{0,2,1:T(8,128)(2,1)S(1)}, bf16[128,2,1024]{0,2,1:T(8,128)(2,1)S(1)}, u32[]{:S(2)}, u32[]{:S(2)}) collective-permute-start(bf16[128,2,1024]{0,2,1:T(8,128)(2,1)S(1)} %get-tuple-element.102), channel_id=1, source_target_pairs={{4,0},{6,2},{8,4},{10,6},{12,8},{14,10},{16,12},{18,14},{20,16},{2... | collective-permute-start | bytes 1572872 | tf_op jit(solution)/shard_map/ppermute | solution.py:18
  209.6 57.7 %collective-permute-start.21 = (bf16[128,2,1024]{0,2,1:T(8,128)(2,1)}, bf16[128,2,1024]{0,2,1:T(8,128)(2,1)}, u32[]{:S(2)}, u32[]{:S(2)}) collective-permute-start(bf16[128,2,1024]{0,2,1:T(8,128)(2,1)} %get-tuple-element.92), channel_id=1, source_target_pairs={{0,8},{2,10},{4,12},{6,14},{8,16},{10,18},{12,20},{14,22},{16,24},... | collective-permute-start | bytes 1572872 | tf_op jit(solution)/shard_map/ppermute | solution.py:18
  220.7 34.5 %collective-permute-start.19 = (bf16[128,2,1024]{0,2,1:T(8,128)(2,1)}, bf16[128,2,1024]{0,2,1:T(8,128)(2,1)S(1)}, u32[]{:S(2)}, u32[]{:S(2)}) collective-permute-start(bf16[128,2,1024]{0,2,1:T(8,128)(2,1)} %get-tuple-element.92), channel_id=1, source_target_pairs={{10,0},{12,2},{14,4},{16,6},{18,8},{20,10},{22,12},{24,14},{26,16}... | collective-permute-start | bytes 1572872 | tf_op jit(solution)/shard_map/ppermute | solution.py:18
  224.4 82.4 %collective-permute-start.16 = (bf16[128,4,1024]{0,2,1:T(8,128)(2,1)}, bf16[128,4,1024]{0,2,1:T(8,128)(2,1)S(1)}, u32[]{:S(2)}, u32[]{:S(2)}) collective-permute-start(bf16[128,4,1024]{0,2,1:T(8,128)(2,1)} %get-tuple-element.45), channel_id=1, source_target_pairs={{6,0},{8,2},{10,4},{12,6},{14,8},{16,10},{18,12},{20,14},{22,16},{... | collective-permute-start | bytes 3145736 | tf_op jit(solution)/shard_map/ppermute | solution.py:18
  231.9 25.9 %copy-start.29 = (bf16[128,2,1024]{0,2,1:T(8,128)(2,1)}, bf16[128,2,1024]{0,2,1:T(8,128)(2,1)S(1)}, u32[]{:S(2)}) copy-start(bf16[128,2,1024]{0,2,1:T(8,128)(2,1)S(1)} %collective-permute-done.18) | copy-start | bytes 1572868
  231.9 74.5 %collective-permute-start.17 = (bf16[128,4,1024]{0,2,1:T(8,128)(2,1)}, bf16[128,4,1024]{0,2,1:T(8,128)(2,1)S(1)}, u32[]{:S(2)}, u32[]{:S(2)}) collective-permute-start(bf16[128,4,1024]{0,2,1:T(8,128)(2,1)} %get-tuple-element.45), channel_id=1, source_target_pairs={{0,6},{2,8},{4,10},{6,12},{8,14},{10,16},{12,18},{14,20},{16,22},{... | collective-permute-start | bytes 3145736 | tf_op jit(solution)/shard_map/ppermute | solution.py:18
  255.1 10.1 %collective-permute-start.26 = (f32[8408]{0:T(1024)S(1)}, f32[8408]{0:T(1024)S(1)}, u32[]{:S(2)}, u32[]{:S(2)}) collective-permute-start(f32[8408]{0:T(1024)S(1)} %get-tuple-element.40), channel_id=1, source_target_pairs={{0,16},{2,18},{4,20},{6,22},{8,24},{10,26},{12,28},{14,30},{16,0},... | collective-permute-start | bytes 100904 | tf_op jit(solution)/shard_map/ppermute | solution.py:89
  265.2 37.7 %collective-permute-start.10 = (bf16[128,4,1024]{0,2,1:T(8,128)(2,1)}, bf16[128,4,1024]{0,2,1:T(8,128)(2,1)}, u32[]{:S(2)}, u32[]{:S(2)}) collective-permute-start(bf16[128,4,1024]{0,2,1:T(8,128)(2,1)} %dynamic-slice_bitcast_fusion), channel_id=1, source_target_pairs={{0,1},{1,0},{2,3},{3,2},{4,5},{5,4},{6,7},{7,6},{8,9},{9,8},{10,11... | collective-permute-start | bytes 3145736 | tf_op jit(solution)/shard_map/ppermute | solution.py:97
  267.1 3.6 %collective-permute-start.27 = (f32[16816]{0:T(1024)S(1)}, f32[16816]{0:T(1024)S(1)}, u32[]{:S(2)}, u32[]{:S(2)}) collective-permute-start(f32[16816]{0:T(1024)S(1)} %dynamic_update_slice.33), channel_id=1, source_target_pairs={{0,8},{2,10},{4,12},{6,14},{8,0},{10,2},{12,4},{14,6},{16,24},{18,... | collective-permute-start | bytes 201800 | tf_op jit(solution)/shard_map/ppermute | solution.py:89
  271.4 14.5 %collective-permute-start.28 = (f32[33632]{0:T(1024)S(1)}, f32[33632]{0:T(1024)S(1)}, u32[]{:S(2)}, u32[]{:S(2)}) collective-permute-start(f32[33632]{0:T(1024)S(1)} %dynamic_update_slice.35), channel_id=1, source_target_pairs={{0,4},{2,6},{4,0},{6,2},{8,12},{10,14},{12,8},{14,10},{16,20},{18,... | collective-permute-start | bytes 403592 | tf_op jit(solution)/shard_map/ppermute | solution.py:89
  287.1 9.0 %collective-permute-start.29 = (f32[67264]{0:T(1024)S(1)}, f32[67264]{0:T(1024)}, u32[]{:S(2)}, u32[]{:S(2)}) collective-permute-start(f32[67264]{0:T(1024)S(1)} %dynamic_update_slice.37), channel_id=1, source_target_pairs={{0,2},{2,0},{4,6},{6,4},{8,10},{10,8},{12,14},{14,12},{16,18},{18,... | collective-permute-start | bytes 807176 | tf_op jit(solution)/shard_map/ppermute | solution.py:89
  (92 other events, 243.6 us)
where the time goes:
time: 324 us; the launch traced here: 318 us
  starting transfers between devices  115 us (35%)
  local copies, waits for them, and re-layouts  74.8 us (23%)
  other arithmetic  64.4 us (20%)
  waiting for transfers between devices  48.6 us (15%)
  matrix products  12.2 us (4%)
    ppermute x20, starting transfers between devices, shifted(): return lax.ppermute(block, axis, route)  86.8 us
    unnamed x227, local copies, waits for them, and re-layouts  23.6 us
    reduce_sum x4, other arithmetic, block(): jnp.sum(grad_f * jnp.roll(feat_rows[row_step * spacing], -col_step * spac...  18.7 us
    ppermute x4, waiting for transfers between devices, band_allreduce(): acc = acc + lax.ppermute(give, 'band', rotate(stride, radix, u))  17.8 us
    ppermute x20, waiting for transfers between devices, shifted(): return lax.ppermute(block, axis, route)  17.6 us
    another operation x3, other arithmetic, block(): stacked = jnp.stack(branches)  16.6 us
    ppermute x4, starting transfers between devices, band_allreduce(): got = lax.ppermute(flat, 'band', rotate(stride, radix, u))  13.8 us
    ppermute x4, starting transfers between devices, band_allreduce(): acc = acc + lax.ppermute(give, 'band', rotate(stride, radix, u))  11.9 us
  transfers between devices with their start and end apart: 30, of which 7 were waited for; matrix products, arithmetic and copies ran while one was open for 28% of the time, Pallas kernels for 0%

commit v1 on v0

--- a/solution.py
+++ b/solution.py
@@ -51,6 +51,9 @@
     count = lax.axis_size("band")
     radices = []
     rest = count
+    while rest % 4 == 0:
+        radices.append(4)
+        rest //= 4
     while rest % 2 == 0:
         radices.append(2)
         rest //= 2
@@ -192,12 +195,12 @@
     for which, spacing in enumerate(dilations):
         grad_input = lax.optimization_barrier(grad_input)
         for row_step in (-1, 1):
-            rows = grad_halo[(which, -row_step * spacing)].astype(jnp.float32)
+            rows = grad_halo[(which, -row_step * spacing)]
             for col_step in (-1, 0, 1):
                 tap_index = (row_step + 1) * 3 + col_step + 1
                 grad_input = grad_input + kernel[which, tap_index][:, None, None] * jnp.roll(
                     rows, col_step * spacing, axis=-1
-                )
+                ).astype(jnp.float32)
     return (output, grad_input, depth_total / GSCALE, point_total / GSCALE)
 
 

time: 324 us -> 310 us (0.957)
  the two profiles are of different devices: /device:TPU:3 before, /device:TPU:9 now
where the time goes in v1:
time: 310 us; the launch traced here: 305 us
  starting transfers between devices  100 us (32%)
  waiting for transfers between devices  67.3 us (22%)
  local copies, waits for them, and re-layouts  63.1 us (20%)
  other arithmetic  57.3 us (18%)
  matrix products  13.4 us (4%)
  between operations  3.15 us (1%)
    ppermute x20, starting transfers between devices, shifted(): return lax.ppermute(block, axis, route)  81 us
    ppermute x20, waiting for transfers between devices, shifted(): return lax.ppermute(block, axis, route)  42.2 us
    unnamed x261, local copies, waits for them, and re-layouts  19.8 us
    reduce_sum x4, other arithmetic, block(): jnp.sum(grad_f * jnp.roll(feat_rows[row_step * spacing], -col_step * spac...  18.2 us
    ppermute x2, waiting for transfers between devices, chan_shift(): lax.ppermute(block, 'chan', [(j, (j + s) % count) for j in range(count)])  17.3 us
    another operation x3, other arithmetic, block(): stacked = jnp.stack(branches)  16 us
    slice x18, local copies, waits for them, and re-layouts, block(): jnp.roll(feat_rows[row_step * spacing], -col_step * spacing, axis=-1)  11.1 us
    ppermute x6, starting transfers between devices, band_allreduce(): got = lax.ppermute(flat, 'band', rotate(stride, radix, u))  9.46 us
  transfers between devices with their start and end apart: 34, of which 9 were waited for; matrix products, arithmetic and copies ran while one was open for 38% of the time, Pallas kernels for 0%

profile of v1, /device:TPU:9, one launch (start us, length us, event | category | flops | bytes accessed | tf_op | source)
XLA Modules:
  0.0 304.5 jit_solution(4151423899605154734)
XLA Ops:
  5.6 5.1 %collective-permute-start.6 = (bf16[128,2,1024]{0,2,1:T(8,128)(2,1)}, bf16[128,2,1024]{0,2,1:T(8,128)(2,1)}, u32[]{:S(2)}, u32[]{:S(2)}) collective-permute-start(bf16[128,2,1024]{0,2,1:T(8,128)(2,1)} %get-tuple-element.123), channel_id=1, source_target_pairs={{0,10},{2,12},{4,14},{6,16},{8,18},{10,20},{12,22},{14,24},{16,26}... | collective-permute-start | bytes 1572872 | tf_op jit(solution)/shard_map/ppermute | solution.py:18
  12.6 4.0 %collective-permute-start = (bf16[128,2,1024]{0,2,1:T(8,128)(2,1)}, bf16[128,2,1024]{0,2,1:T(8,128)(2,1)}, u32[]{:S(2)}, u32[]{:S(2)}) collective-permute-start(bf16[128,2,1024]{0,2,1:T(8,128)(2,1)} %get-tuple-element.123), channel_id=1, source_target_pairs={{0,4},{2,6},{4,8},{6,10},{8,12},{10,14},{12,16},{14,18},{16,20},{1... | collective-permute-start | bytes 1572872 | tf_op jit(solution)/shard_map/ppermute | solution.py:18
  19.9 2.3 fusion.114
  22.1 2.3 fusion.110
  27.5 2.5 copy.33
  30.0 2.5 fusion.60
  32.6 4.6 %collective-permute-start.9 = (bf16[128,2,1024]{0,2,1:T(8,128)(2,1)}, bf16[128,2,1024]{0,2,1:T(8,128)(2,1)S(1)}, u32[]{:S(2)}, u32[]{:S(2)}) collective-permute-start(bf16[128,2,1024]{0,2,1:T(8,128)(2,1)} %get-tuple-element.124), channel_id=1, source_target_pairs={{10,0},{12,2},{14,4},{16,6},{18,8},{20,10},{22,12},{24,14},{26,16}... | collective-permute-start | bytes 1572872 | tf_op jit(solution)/shard_map/ppermute | solution.py:18
  37.1 9.9 %collective-permute-start.3 = (bf16[128,2,1024]{0,2,1:T(8,128)(2,1)}, bf16[128,2,1024]{0,2,1:T(8,128)(2,1)S(1)}, u32[]{:S(2)}, u32[]{:S(2)}) collective-permute-start(bf16[128,2,1024]{0,2,1:T(8,128)(2,1)} %get-tuple-element.124), channel_id=1, source_target_pairs={{4,0},{6,2},{8,4},{10,6},{12,8},{14,10},{16,12},{18,14},{20,16},{2... | collective-permute-start | bytes 1572872 | tf_op jit(solution)/shard_map/ppermute | solution.py:18
  48.4 2.2 fusion.88
  50.6 6.3 %collective-permute-start.1 = (bf16[128,2,1024]{0,2,1:T(8,128)(2,1)}, bf16[128,2,1024]{0,2,1:T(8,128)(2,1)S(1)}, u32[]{:S(2)}, u32[]{:S(2)}) collective-permute-start(bf16[128,2,1024]{0,2,1:T(8,128)(2,1)} %get-tuple-element.124), channel_id=1, source_target_pairs={{0,2},{2,4},{4,6},{6,8},{8,10},{10,12},{12,14},{14,16},{16,18},{18... | collective-permute-start | bytes 1572872 | tf_op jit(solution)/shard_map/ppermute | solution.py:18
  60.4 5.1 %collective-permute-start.4 = (bf16[128,4,1024]{0,2,1:T(8,128)(2,1)S(1)}, bf16[128,4,1024]{0,2,1:T(8,128)(2,1)S(1)}, u32[]{:S(2)}, u32[]{:S(2)}) collective-permute-start(bf16[128,4,1024]{0,2,1:T(8,128)(2,1)S(1)} %copy.25), channel_id=1, source_target_pairs={{0,6},{2,8},{4,10},{6,12},{8,14},{10,16},{12,18},{14,20},{16,22},{... | collective-permute-start | bytes 3145736 | tf_op jit(solution)/shard_map/ppermute | solution.py:18
  65.5 8.9 %collective-permute-done.3 = bf16[128,2,1024]{0,2,1:T(8,128)(2,1)S(1)} collective-permute-done((bf16[128,2,1024]{0,2,1:T(8,128)(2,1)}, bf16[128,2,1024]{0,2,1:T(8,128)(2,1)S(1)}, u32[]{:S(2)}, u32[]{:S(2)}) %collective-permute-start.3) | collective-permute-done | bytes 524320 | tf_op jit(solution)/shard_map/ppermute | solution.py:18
  77.3 11.8 %collective-permute-done.1 = bf16[128,2,1024]{0,2,1:T(8,128)(2,1)S(1)} collective-permute-done((bf16[128,2,1024]{0,2,1:T(8,128)(2,1)}, bf16[128,2,1024]{0,2,1:T(8,128)(2,1)S(1)}, u32[]{:S(2)}, u32[]{:S(2)}) %collective-permute-start.1) | collective-permute-done | bytes 524320 | tf_op jit(solution)/shard_map/ppermute | solution.py:18
  90.4 6.1 %fusion.62 = bf16[1,128,4,1024]{1,3,0,2:T(8,128)(2,1)} fusion(f32[128,4,18]{0,2,1:T(8,128)S(1)} %get-tuple-element.72, f32[128,4,1006]{0,2,1:T(8,128)S(1)} %get-tuple-element.74, f32[128]{0:T(128)S(1)} %copy-done.75, f32[128]{0:T(128)S(1)} %copy-done.77, f32[128,4,1006]{0,2,1:T(8,128)S(1)} %get-tuple-element.73, f32[128,4,18]{0,2,1:T(8,128)S(1)} %get-tuple-element.71, ...), kind=kLoop, calls=%fused_computation.137 | loop fusion | flops 15204352 | bytes 16781824 | tf_op jit(solution)/shard_map/stack | solution.py:147
  98.2 5.5 %fusion.64 = bf16[1,128,4,1024]{1,3,0,2:T(8,128)(2,1)} fusion(f32[128,4,6]{0,2,1:T(8,128)S(1)} %get-tuple-element.64, f32[128,4,1018]{0,2,1:T(8,128)S(1)} %get-tuple-element.66, f32[128]{0:T(128)S(1)} %copy-done.103, f32[128]{0:T(128)S(1)} %copy-done.105, f32[128,4,1018]{0,2,1:T(8,128)S(1)} %get-tuple-element.65, f32[128,4,6]{0,2,1:T(8,128)S(1)} %get-tuple-element.63, ...), kind=kLoop, calls=%fused_computation.139 | loop fusion | flops 15204352 | bytes 16781824 | tf_op jit(solution)/shard_map/stack | solution.py:147
  103.8 2.5 add_convert_fusion
  106.3 2.7 fusion.75
  115.5 2.2 fusion.78
  117.7 2.2 fusion.80
  123.0 2.9 fusion.32
  126.0 4.4 %fusion.63 = bf16[1,128,4,1024]{1,3,0,2:T(8,128)(2,1)} fusion(f32[128,4,12]{0,2,1:T(8,128)S(1)} %get-tuple-element.116, f32[128,4,1012]{0,2,1:T(8,128)S(1)} %get-tuple-element.118, f32[128]{0:T(128)S(1)} %copy-done.87, bf16[128,4,1024]{0,2,1:T(8,128)(2,1)S(1)} %collective-permute-done.5, f32[128]{0:T(128)S(1)} %copy-done.89, f32[128,4,1012]{0,2,1:T(8,128)} %copy-done.10, ...), kind=kLoop, calls=%fused_computation.138 | loop fusion | flops 14155776 | bytes 16781824 | tf_op jit(solution)/shard_map/stack | solution.py:147
  130.4 4.0 %bitcast_convert_fusion = bf16[4,1024,256]{2,1,0:T(8,128)(2,1)} fusion(bf16[4,128,256]{2,1,0:T(8,128)(2,1)S(1)} %copy-done, bf16[1,128,4,1024]{1,3,0,2:T(8,128)(2,1)S(1)} %copy-done.33, bf16[1,128,4,1024]{1,3,0,2:T(8,128)(2,1)} %fusion.63, bf16[1,128,4,1024]{1,3,0,2:T(8,128)(2,1)S(1)} %copy-done.34, bf16[1,128,4,1024]{1,3,0,2:T(8,128)(2,1)S(1)} %bitcast.215), kind=kOutput, calls=%fused_computation.32 | convolution fusion | flops 1081081856 | bytes 6553600 | tf_op jit(solution)/shard_map/bchw,bco->ohw/dot_general | solution.py:149
  136.2 2.7 fusion.55
  140.0 4.7 %fusion.30 = (f32[128]{0:T(128)}, f32[128]{0:T(128)}, f32[128]{0:T(128)}, f32[128]{0:T(128)}, f32[128]{0:T(128)}, /*index=5*/f32[128]{0:T(128)}, f32[128]{0:T(128)}, f32[128]{0:T(128)}) fusion(bf16[128,4,1024]{0,2,1:T(8,128)(2,1)S(1)} %copy.25, bf16[4,128,4,1024]{1,3,2,0:T(8,128)(2,1)S(1)} %add_convert_fusion, f32[128,4,6]{0,2,1:T(8,128)S(1)} %copy-done.45, ...), kind=kLoop, calls=%fused_computation.66 | loop fusion | flops 13630464 | bytes 13635584 | tf_op jit(solution)/shard_map/reduce_sum | solution.py:176
  144.8 3.9 %fusion.33 = (f32[128]{0:T(128)S(1)}, f32[128]{0:T(128)S(1)}, f32[128]{0:T(128)S(1)}, f32[128]{0:T(128)S(1)}, f32[128]{0:T(128)S(1)}, /*index=5*/f32[128]{0:T(128)S(1)}, f32[128]{0:T(128)S(1)}) fusion(bf16[128,2,1024]{0,2,1:T(8,128)(2,1)S(1)} %collective-permute-done.3, bf16[128,2,1024]{0,2,1:T(8,128)(2,1)} %collective-permute-done.2, ...), kind=kLoop, calls=%fused_computation.69 | loop fusion | flops 13630592 | bytes 13635072 | tf_op jit(solution)/shard_map/reduce_sum | solution.py:176
  149.0 6.6 %fusion.34 = (f32[128]{0:T(128)S(1)}, f32[128]{0:T(128)S(1)}, f32[128]{0:T(128)S(1)}, f32[128]{0:T(128)S(1)}, f32[128]{0:T(128)S(1)}, /*index=5*/f32[128]{0:T(128)S(1)}) fusion(f32[128,4,6]{0,2,1:T(8,128)S(1)} %copy-done.47, f32[128,4,1018]{0,2,1:T(8,128)} %copy-done.7, bf16[4,128,4,1024]{1,3,2,0:T(8,128)(2,1)} %copy-done.2, ...), kind=kLoop, calls=%fused_computation.70 | loop fusion | flops 11009280 | bytes 13634560 | tf_op jit(solution)/shard_map/reduce_sum | solution.py:176
  157.1 2.0 constant_dynamic-update-slice_fusion.9
  160.3 3.8 %collective-permute-start.22 = (f32[33632]{0:T(1024)S(1)}, f32[33632]{0:T(1024)S(1)}, u32[]{:S(2)}, u32[]{:S(2)}) collective-permute-start(f32[33632]{0:T(1024)S(1)} %get-tuple-element.125), channel_id=1, source_target_pairs={{0,2},{2,4},{4,6},{6,0},{8,10},{10,12},{12,14},{14,8},{16,18},{18,... | collective-permute-start | bytes 403592 | tf_op jit(solution)/shard_map/ppermute | solution.py:83
  166.5 3.6 %collective-permute-done.24 = f32[33632]{0:T(1024)S(1)} collective-permute-done((f32[33632]{0:T(1024)S(1)}, f32[33632]{0:T(1024)S(1)}, u32[]{:S(2)}, u32[]{:S(2)}) %collective-permute-start.24) | collective-permute-done | bytes 134560 | tf_op jit(solution)/shard_map/ppermute | solution.py:83
  174.4 4.6 %fusion.25 = f32[128,4,1024]{0,2,1:T(8,128)} fusion(f32[128,4,6]{0,2,1:T(8,128)S(1)} %get-tuple-element.56, f32[128,4,1018]{0,2,1:T(8,128)S(1)} %get-tuple-element.58, f32[128,4,1018]{0,2,1:T(8,128)S(1)} %get-tuple-element.57, f32[128,4,6]{0,2,1:T(8,128)S(1)} %get-tuple-element.55, f32[128,4,12]{0,2,1:T(8,128)S(1)} %copy-done.55, ...), kind=kLoop, calls=%fused_computation.61 | loop fusion | flops 14680064 | bytes 18878976 | tf_op jit(solution)/shard_map/add | solution.py:192
  179.4 2.4 collective-permute-start.29
  186.3 3.9 %collective-permute-start.33 = (f32[33632]{0:T(1024)S(1)}, f32[33632]{0:T(1024)S(1)}, u32[]{:S(2)}, u32[]{:S(2)}) collective-permute-start(f32[33632]{0:T(1024)S(1)} %dynamic_update_slice.35), channel_id=1, source_target_pairs={{0,6},{2,0},{4,2},{6,4},{8,14},{10,8},{12,10},{14,12},{16,22},{18,... | collective-permute-start | bytes 403592 | tf_op jit(solution)/shard_map/ppermute | solution.py:92
  194.3 2.4 collective-permute-done.31
  196.7 2.2 collective-permute-start.14
  200.1 4.3 %collective-permute-start.12 = (bf16[128,2,1024]{0,2,1:T(8,128)(2,1)}, bf16[128,2,1024]{0,2,1:T(8,128)(2,1)S(1)}, u32[]{:S(2)}, u32[]{:S(2)}) collective-permute-start(bf16[128,2,1024]{0,2,1:T(8,128)(2,1)} %get-tuple-element.100), channel_id=1, source_target_pairs={{2,0},{4,2},{6,4},{8,6},{10,8},{12,10},{14,12},{16,14},{18,16},{20... | collective-permute-start | bytes 1572872 | tf_op jit(solution)/shard_map/ppermute | solution.py:18
  205.5 4.2 %collective-permute-start.13 = (bf16[128,2,1024]{0,2,1:T(8,128)(2,1)}, bf16[128,2,1024]{0,2,1:T(8,128)(2,1)S(1)}, u32[]{:S(2)}, u32[]{:S(2)}) collective-permute-start(bf16[128,2,1024]{0,2,1:T(8,128)(2,1)} %get-tuple-element.99), channel_id=1, source_target_pairs={{4,0},{6,2},{8,4},{10,6},{12,8},{14,10},{16,12},{18,14},{20,16},{2... | collective-permute-start | bytes 1572872 | tf_op jit(solution)/shard_map/ppermute | solution.py:18
  212.6 12.5 %collective-permute-done.14 = bf16[128,2,1024]{0,2,1:T(8,128)(2,1)S(1)} collective-permute-done((bf16[128,2,1024]{0,2,1:T(8,128)(2,1)}, bf16[128,2,1024]{0,2,1:T(8,128)(2,1)S(1)}, u32[]{:S(2)}, u32[]{:S(2)}) %collective-permute-start.14) | collective-permute-done | bytes 524320 | tf_op jit(solution)/shard_map/ppermute | solution.py:18
  225.1 7.6 %collective-permute-start.20 = (bf16[128,2,1024]{0,2,1:T(8,128)(2,1)}, bf16[128,2,1024]{0,2,1:T(8,128)(2,1)S(1)}, u32[]{:S(2)}, u32[]{:S(2)}) collective-permute-start(bf16[128,2,1024]{0,2,1:T(8,128)(2,1)} %get-tuple-element.102), channel_id=1, source_target_pairs={{0,10},{2,12},{4,14},{6,16},{8,18},{10,20},{12,22},{14,24},{16,26}... | collective-permute-start | bytes 1572872 | tf_op jit(solution)/shard_map/ppermute | solution.py:18
  232.8 2.5 collective-permute-start.18
  235.3 2.8 collective-permute-start.15
  238.6 9.0 %collective-permute-done.15 = bf16[128,2,1024]{0,2,1:T(8,128)(2,1)S(1)} collective-permute-done((bf16[128,2,1024]{0,2,1:T(8,128)(2,1)}, bf16[128,2,1024]{0,2,1:T(8,128)(2,1)S(1)}, u32[]{:S(2)}, u32[]{:S(2)}) %collective-permute-start.15) | collective-permute-done | bytes 524320 | tf_op jit(solution)/shard_map/ppermute | solution.py:18
  251.2 2.7 multiply_add_fusion.2
  253.9 9.0 %collective-permute-start.17 = (bf16[128,4,1024]{0,2,1:T(8,128)(2,1)}, bf16[128,4,1024]{0,2,1:T(8,128)(2,1)}, u32[]{:S(2)}, u32[]{:S(2)}) collective-permute-start(bf16[128,4,1024]{0,2,1:T(8,128)(2,1)} %get-tuple-element.45), channel_id=1, source_target_pairs={{0,6},{2,8},{4,10},{6,12},{8,14},{10,16},{12,18},{14,20},{16,22},{... | collective-permute-start | bytes 3145736 | tf_op jit(solution)/shard_map/ppermute | solution.py:18
  270.0 17.3 %collective-permute-done.10 = bf16[128,4,1024]{0,2,1:T(8,128)(2,1)S(1)} collective-permute-done((bf16[128,4,1024]{0,2,1:T(8,128)(2,1)S(1)}, bf16[128,4,1024]{0,2,1:T(8,128)(2,1)S(1)}, u32[]{:S(2)}, u32[]{:S(2)}) %collective-permute-start.10) | collective-permute-done | bytes 1048608 | tf_op jit(solution)/shard_map/ppermute | solution.py:100
  288.6 2.6 copy.40
  295.5 2.9 multiply_add_fusion.1
  298.6 2.7 multiply_add_fusion
  301.2 3.0 copy.41
  (375 shorter events, 75.3 us)
Async XLA Ops:
  0.6 29.4 %copy-start = (bf16[4,128,256]{2,1,0:T(8,128)(2,1)S(1)}, bf16[4,128,256]{2,1,0:T(8,128)(2,1)}, u32[]{:S(2)}) copy-start(bf16[4,128,256]{2,1,0:T(8,128)(2,1)} %param.6) | copy-start | bytes 786436
  3.7 46.9 %collective-permute-start.8 = (bf16[128,2,1024]{0,2,1:T(8,128)(2,1)}, bf16[128,2,1024]{0,2,1:T(8,128)(2,1)}, u32[]{:S(2)}, u32[]{:S(2)}) collective-permute-start(bf16[128,2,1024]{0,2,1:T(8,128)(2,1)} %get-tuple-element.123), channel_id=1, source_target_pairs={{8,0},{10,2},{12,4},{14,6},{16,8},{18,10},{20,12},{22,14},{24,16},... | collective-permute-start | bytes 1572872 | tf_op jit(solution)/shard_map/ppermute | solution.py:18
  5.6 27.0 %collective-permute-start.6 = (bf16[128,2,1024]{0,2,1:T(8,128)(2,1)}, bf16[128,2,1024]{0,2,1:T(8,128)(2,1)}, u32[]{:S(2)}, u32[]{:S(2)}) collective-permute-start(bf16[128,2,1024]{0,2,1:T(8,128)(2,1)} %get-tuple-element.123), channel_id=1, source_target_pairs={{0,10},{2,12},{4,14},{6,16},{8,18},{10,20},{12,22},{14,24},{16,26}... | collective-permute-start | bytes 1572872 | tf_op jit(solution)/shard_map/ppermute | solution.py:18
  10.7 49.7 %collective-permute-start.2 = (bf16[128,2,1024]{0,2,1:T(8,128)(2,1)}, bf16[128,2,1024]{0,2,1:T(8,128)(2,1)}, u32[]{:S(2)}, u32[]{:S(2)}) collective-permute-start(bf16[128,2,1024]{0,2,1:T(8,128)(2,1)} %get-tuple-element.123), channel_id=1, source_target_pairs={{2,0},{4,2},{6,4},{8,6},{10,8},{12,10},{14,12},{16,14},{18,16},{20... | collective-permute-start | bytes 1572872 | tf_op jit(solution)/shard_map/ppermute | solution.py:18
  12.6 64.6 %collective-permute-start = (bf16[128,2,1024]{0,2,1:T(8,128)(2,1)}, bf16[128,2,1024]{0,2,1:T(8,128)(2,1)}, u32[]{:S(2)}, u32[]{:S(2)}) collective-permute-start(bf16[128,2,1024]{0,2,1:T(8,128)(2,1)} %get-tuple-element.123), channel_id=1, source_target_pairs={{0,4},{2,6},{4,8},{6,10},{8,12},{10,14},{12,16},{14,18},{16,20},{1... | collective-permute-start | bytes 1572872 | tf_op jit(solution)/shard_map/ppermute | solution.py:18
  16.7 20.5 %collective-permute-start.7 = (bf16[128,2,1024]{0,2,1:T(8,128)(2,1)}, bf16[128,2,1024]{0,2,1:T(8,128)(2,1)}, u32[]{:S(2)}, u32[]{:S(2)}) collective-permute-start(bf16[128,2,1024]{0,2,1:T(8,128)(2,1)} %get-tuple-element.124), channel_id=1, source_target_pairs={{0,8},{2,10},{4,12},{6,14},{8,16},{10,18},{12,20},{14,22},{16,24},... | collective-permute-start | bytes 1572872 | tf_op jit(solution)/shard_map/ppermute | solution.py:18
  26.1 70.9 %copy-start.4 = (f32[128,4,1018]{0,2,1:T(8,128)}, f32[128,4,1018]{0,2,1:T(8,128)S(1)}, u32[]{:S(2)}) copy-start(f32[128,4,1018]{0,2,1:T(8,128)S(1)} %get-tuple-element.105) | copy-start | bytes 6254596
  32.6 24.4 %collective-permute-start.9 = (bf16[128,2,1024]{0,2,1:T(8,128)(2,1)}, bf16[128,2,1024]{0,2,1:T(8,128)(2,1)S(1)}, u32[]{:S(2)}, u32[]{:S(2)}) collective-permute-start(bf16[128,2,1024]{0,2,1:T(8,128)(2,1)} %get-tuple-element.124), channel_id=1, source_target_pairs={{10,0},{12,2},{14,4},{16,6},{18,8},{20,10},{22,12},{24,14},{26,16}... | collective-permute-start | bytes 1572872 | tf_op jit(solution)/shard_map/ppermute | solution.py:18
  37.1 37.3 %collective-permute-start.3 = (bf16[128,2,1024]{0,2,1:T(8,128)(2,1)}, bf16[128,2,1024]{0,2,1:T(8,128)(2,1)S(1)}, u32[]{:S(2)}, u32[]{:S(2)}) collective-permute-start(bf16[128,2,1024]{0,2,1:T(8,128)(2,1)} %get-tuple-element.124), channel_id=1, source_target_pairs={{4,0},{6,2},{8,4},{10,6},{12,8},{14,10},{16,12},{18,14},{20,16},{2... | collective-permute-start | bytes 1572872 | tf_op jit(solution)/shard_map/ppermute | solution.py:18
  50.6 38.5 %collective-permute-start.1 = (bf16[128,2,1024]{0,2,1:T(8,128)(2,1)}, bf16[128,2,1024]{0,2,1:T(8,128)(2,1)S(1)}, u32[]{:S(2)}, u32[]{:S(2)}) collective-permute-start(bf16[128,2,1024]{0,2,1:T(8,128)(2,1)} %get-tuple-element.124), channel_id=1, source_target_pairs={{0,2},{2,4},{4,6},{6,8},{8,10},{10,12},{12,14},{14,16},{16,18},{18... | collective-permute-start | bytes 1572872 | tf_op jit(solution)/shard_map/ppermute | solution.py:18
  56.9 33.4 %copy-start.22 = (bf16[128,2,1024]{0,2,1:T(8,128)(2,1)}, bf16[128,2,1024]{0,2,1:T(8,128)(2,1)S(1)}, u32[]{:S(2)}) copy-start(bf16[128,2,1024]{0,2,1:T(8,128)(2,1)S(1)} %collective-permute-done.9) | copy-start | bytes 1572868
  56.9 63.0 %collective-permute-start.5 = (bf16[128,4,1024]{0,2,1:T(8,128)(2,1)S(1)}, bf16[128,4,1024]{0,2,1:T(8,128)(2,1)S(1)}, u32[]{:S(2)}, u32[]{:S(2)}) collective-permute-start(bf16[128,4,1024]{0,2,1:T(8,128)(2,1)S(1)} %copy.25), channel_id=1, source_target_pairs={{6,0},{8,2},{10,4},{12,6},{14,8},{16,10},{18,12},{20,14},{22,16},{... | collective-permute-start | bytes 3145736 | tf_op jit(solution)/shard_map/ppermute | solution.py:18
  60.1 30.2 %copy-start.38 = (f32[128,4,18]{0,2,1:T(8,128)}, f32[128,4,18]{0,2,1:T(8,128)S(1)}, u32[]{:S(2)}) copy-start(f32[128,4,18]{0,2,1:T(8,128)S(1)} %get-tuple-element.72) | copy-start | bytes 110596
  60.4 29.9 %copy-start.13 = (f32[128,4,1006]{0,2,1:T(8,128)}, f32[128,4,1006]{0,2,1:T(8,128)S(1)}, u32[]{:S(2)}) copy-start(f32[128,4,1006]{0,2,1:T(8,128)S(1)} %get-tuple-element.73) | copy-start | bytes 6180868
  60.4 29.9 %copy-start.14 = (f32[128,4,1006]{0,2,1:T(8,128)}, f32[128,4,1006]{0,2,1:T(8,128)S(1)}, u32[]{:S(2)}) copy-start(f32[128,4,1006]{0,2,1:T(8,128)S(1)} %get-tuple-element.74) | copy-start | bytes 6180868
  60.4 54.1 %collective-permute-start.4 = (bf16[128,4,1024]{0,2,1:T(8,128)(2,1)S(1)}, bf16[128,4,1024]{0,2,1:T(8,128)(2,1)S(1)}, u32[]{:S(2)}, u32[]{:S(2)}) collective-permute-start(bf16[128,4,1024]{0,2,1:T(8,128)(2,1)S(1)} %copy.25), channel_id=1, source_target_pairs={{0,6},{2,8},{4,10},{6,12},{8,14},{10,16},{12,18},{14,20},{16,22},{... | collective-permute-start | bytes 3145736 | tf_op jit(solution)/shard_map/ppermute | solution.py:18
  74.4 29.4 %collective-permute-start.11 = (bf16[128,4,1024]{2,0,1:T(8,128)(2,1)}, bf16[128,4,1024]{2,0,1:T(8,128)(2,1)}, u32[]{:S(2)}, u32[]{:S(2)}) collective-permute-start(bf16[128,4,1024]{2,0,1:T(8,128)(2,1)} %copy.33), channel_id=1, source_target_pairs={{0,1},{1,0},{2,3},{3,2},{4,5},{5,4},{6,7},{7,6},{8,9},{9,8},{10,11... | collective-permute-start | bytes 3145736 | tf_op jit(solution)/shard_map/ppermute | solution.py:100
  76.8 20.1 %copy-start.46 = (f32[128,4,6]{0,2,1:T(8,128)}, f32[128,4,6]{0,2,1:T(8,128)S(1)}, u32[]{:S(2)}) copy-start(f32[128,4,6]{0,2,1:T(8,128)S(1)} %get-tuple-element.64) | copy-start | bytes 36868
  76.8 20.1 %copy-start.52 = (f32[128,4,6]{0,2,1:T(8,128)}, f32[128,4,6]{0,2,1:T(8,128)S(1)}, u32[]{:S(2)}) copy-start(f32[128,4,6]{0,2,1:T(8,128)S(1)} %get-tuple-element.63) | copy-start | bytes 36868
  76.9 13.5 %copy-start.12 = (f32[128,4,1006]{0,2,1:T(8,128)S(1)}, f32[128,4,1006]{0,2,1:T(8,128)}, u32[]{:S(2)}) copy-start(f32[128,4,1006]{0,2,1:T(8,128)} %get-tuple-element.122) | copy-start | bytes 6180868
  77.2 19.8 %copy-start.7 = (f32[128,4,1018]{0,2,1:T(8,128)}, f32[128,4,1018]{0,2,1:T(8,128)S(1)}, u32[]{:S(2)}) copy-start(f32[128,4,1018]{0,2,1:T(8,128)S(1)} %get-tuple-element.66) | copy-start | bytes 6254596
  77.2 13.2 %copy-start.11 = (f32[128,4,1006]{0,2,1:T(8,128)S(1)}, f32[128,4,1006]{0,2,1:T(8,128)}, u32[]{:S(2)}) copy-start(f32[128,4,1006]{0,2,1:T(8,128)} %get-tuple-element.121) | copy-start | bytes 6180868
  106.3 38.4 %copy-start.2 = (bf16[4,128,4,1024]{1,3,2,0:T(8,128)(2,1)}, bf16[4,128,4,1024]{1,3,2,0:T(8,128)(2,1)S(1)}, u32[]{:S(2)}) copy-start(bf16[4,128,4,1024]{1,3,2,0:T(8,128)(2,1)S(1)} %add_convert_fusion) | copy-start | bytes 12582916
  110.1 157.1 %collective-permute-start.21 = (bf16[128,2,1024]{0,2,1:T(8,128)(2,1)}, bf16[128,2,1024]{0,2,1:T(8,128)(2,1)}, u32[]{:S(2)}, u32[]{:S(2)}) collective-permute-start(bf16[128,2,1024]{0,2,1:T(8,128)(2,1)} %get-tuple-element.101), channel_id=1, source_target_pairs={{0,8},{2,10},{4,12},{6,14},{8,16},{10,18},{12,20},{14,22},{16,24},... | collective-permute-start | bytes 1572872 | tf_op jit(solution)/shard_map/ppermute | solution.py:18
  112.0 151.0 %collective-permute-start.19 = (bf16[128,2,1024]{0,2,1:T(8,128)(2,1)}, bf16[128,2,1024]{0,2,1:T(8,128)(2,1)}, u32[]{:S(2)}, u32[]{:S(2)}) collective-permute-start(bf16[128,2,1024]{0,2,1:T(8,128)(2,1)} %get-tuple-element.101), channel_id=1, source_target_pairs={{10,0},{12,2},{14,4},{16,6},{18,8},{20,10},{22,12},{24,14},{26,16}... | collective-permute-start | bytes 1572872 | tf_op jit(solution)/shard_map/ppermute | solution.py:18
  157.1 17.2 %copy-start.21 = (f32[128,4,1006]{0,2,1:T(8,128)S(1)}, f32[128,4,1006]{0,2,1:T(8,128)}, u32[]{:S(2)}) copy-start(f32[128,4,1006]{0,2,1:T(8,128)} %get-tuple-element.49) | copy-start | bytes 6180868
  160.3 6.2 %collective-permute-start.22 = (f32[33632]{0:T(1024)S(1)}, f32[33632]{0:T(1024)S(1)}, u32[]{:S(2)}, u32[]{:S(2)}) collective-permute-start(f32[33632]{0:T(1024)S(1)} %get-tuple-element.125), channel_id=1, source_target_pairs={{0,2},{2,4},{4,6},{6,0},{8,10},{10,12},{12,14},{14,8},{16,18},{18,... | collective-permute-start | bytes 403592 | tf_op jit(solution)/shard_map/ppermute | solution.py:83
  164.1 6.0 %collective-permute-start.24 = (f32[33632]{0:T(1024)S(1)}, f32[33632]{0:T(1024)S(1)}, u32[]{:S(2)}, u32[]{:S(2)}) collective-permute-start(f32[33632]{0:T(1024)S(1)} %get-tuple-element.126), channel_id=1, source_target_pairs={{0,6},{2,0},{4,2},{6,4},{8,14},{10,8},{12,10},{14,12},{16,22},{18,... | collective-permute-start | bytes 403592 | tf_op jit(solution)/shard_map/ppermute | solution.py:83
  164.2 7.4 %collective-permute-start.23 = (f32[33632]{0:T(1024)S(1)}, f32[33632]{0:T(1024)S(1)}, u32[]{:S(2)}, u32[]{:S(2)}) collective-permute-start(f32[33632]{0:T(1024)S(1)} %get-tuple-element.127), channel_id=1, source_target_pairs={{0,4},{2,6},{4,0},{6,2},{8,12},{10,14},{12,8},{14,10},{16,20},{18,... | collective-permute-start | bytes 403592 | tf_op jit(solution)/shard_map/ppermute | solution.py:83
  172.7 6.3 %collective-permute-start.25 = (f32[8408]{0:T(1024)S(1)}, f32[8408]{0:T(1024)S(1)}, u32[]{:S(2)}, u32[]{:S(2)}) collective-permute-start(f32[8408]{0:T(1024)S(1)} %get-tuple-element.128), channel_id=1, source_target_pairs={{0,8},{2,10},{4,12},{6,14},{8,16},{10,18},{12,20},{14,22},{16,24},... | collective-permute-start | bytes 100904 | tf_op jit(solution)/shard_map/ppermute | solution.py:83
  172.8 6.3 %collective-permute-start.27 = (f32[8408]{0:T(1024)S(1)}, f32[8408]{0:T(1024)S(1)}, u32[]{:S(2)}, u32[]{:S(2)}) collective-permute-start(f32[8408]{0:T(1024)S(1)} %get-tuple-element.129), channel_id=1, source_target_pairs={{0,24},{2,26},{4,28},{6,30},{8,0},{10,2},{12,4},{14,6},{16,8},{18,... | collective-permute-start | bytes 100904 | tf_op jit(solution)/shard_map/ppermute | solution.py:83
  174.3 4.8 %collective-permute-start.26 = (f32[8408]{0:T(1024)S(1)}, f32[8408]{0:T(1024)S(1)}, u32[]{:S(2)}, u32[]{:S(2)}) collective-permute-start(f32[8408]{0:T(1024)S(1)} %get-tuple-element.130), channel_id=1, source_target_pairs={{0,16},{2,18},{4,20},{6,22},{8,24},{10,26},{12,28},{14,30},{16,0},... | collective-permute-start | bytes 100904 | tf_op jit(solution)/shard_map/ppermute | solution.py:83
  179.4 5.8 %collective-permute-start.29 = (f32[8408]{0:T(1024)S(1)}, f32[8408]{0:T(1024)S(1)}, u32[]{:S(2)}, u32[]{:S(2)}) collective-permute-start(f32[8408]{0:T(1024)S(1)} %get-tuple-element.40), channel_id=1, source_target_pairs={{0,16},{2,18},{4,20},{6,22},{8,24},{10,26},{12,28},{14,30},{16,0},... | collective-permute-start | bytes 100904 | tf_op jit(solution)/shard_map/ppermute | solution.py:92
  181.8 2.8 collective-permute-start.28
  181.9 3.8 %collective-permute-start.30 = (f32[8408]{0:T(1024)S(1)}, f32[8408]{0:T(1024)S(1)}, u32[]{:S(2)}, u32[]{:S(2)}) collective-permute-start(f32[8408]{0:T(1024)S(1)} %get-tuple-element.40), channel_id=1, source_target_pairs={{0,24},{2,26},{4,28},{6,30},{8,0},{10,2},{12,4},{14,6},{16,8},{18,... | collective-permute-start | bytes 100904 | tf_op jit(solution)/shard_map/ppermute | solution.py:92
  186.3 19.2 %collective-permute-start.33 = (f32[33632]{0:T(1024)S(1)}, f32[33632]{0:T(1024)S(1)}, u32[]{:S(2)}, u32[]{:S(2)}) collective-permute-start(f32[33632]{0:T(1024)S(1)} %dynamic_update_slice.35), channel_id=1, source_target_pairs={{0,6},{2,0},{4,2},{6,4},{8,14},{10,8},{12,10},{14,12},{16,22},{18,... | collective-permute-start | bytes 403592 | tf_op jit(solution)/shard_map/ppermute | solution.py:92
  190.2 10.0 %collective-permute-start.32 = (f32[33632]{0:T(1024)S(1)}, f32[33632]{0:T(1024)S(1)}, u32[]{:S(2)}, u32[]{:S(2)}) collective-permute-start(f32[33632]{0:T(1024)S(1)} %dynamic_update_slice.35), channel_id=1, source_target_pairs={{0,4},{2,6},{4,0},{6,2},{8,12},{10,14},{12,8},{14,10},{16,20},{18,... | collective-permute-start | bytes 403592 | tf_op jit(solution)/shard_map/ppermute | solution.py:92
  190.5 6.2 %collective-permute-start.31 = (f32[33632]{0:T(1024)S(1)}, f32[33632]{0:T(1024)S(1)}, u32[]{:S(2)}, u32[]{:S(2)}) collective-permute-start(f32[33632]{0:T(1024)S(1)} %dynamic_update_slice.35), channel_id=1, source_target_pairs={{0,2},{2,4},{4,6},{6,0},{8,10},{10,12},{12,14},{14,8},{16,18},{18,... | collective-permute-start | bytes 403592 | tf_op jit(solution)/shard_map/ppermute | solution.py:92
  196.7 28.4 %collective-permute-start.14 = (bf16[128,2,1024]{0,2,1:T(8,128)(2,1)}, bf16[128,2,1024]{0,2,1:T(8,128)(2,1)S(1)}, u32[]{:S(2)}, u32[]{:S(2)}) collective-permute-start(bf16[128,2,1024]{0,2,1:T(8,128)(2,1)} %get-tuple-element.100), channel_id=1, source_target_pairs={{0,4},{2,6},{4,8},{6,10},{8,12},{10,14},{12,16},{14,18},{16,20},{1... | collective-permute-start | bytes 1572872 | tf_op jit(solution)/shard_map/ppermute | solution.py:18
  200.1 32.6 %collective-permute-start.12 = (bf16[128,2,1024]{0,2,1:T(8,128)(2,1)}, bf16[128,2,1024]{0,2,1:T(8,128)(2,1)S(1)}, u32[]{:S(2)}, u32[]{:S(2)}) collective-permute-start(bf16[128,2,1024]{0,2,1:T(8,128)(2,1)} %get-tuple-element.100), channel_id=1, source_target_pairs={{2,0},{4,2},{6,4},{8,6},{10,8},{12,10},{14,12},{16,14},{18,16},{20... | collective-permute-start | bytes 1572872 | tf_op jit(solution)/shard_map/ppermute | solution.py:18
  205.5 29.8 %collective-permute-start.13 = (bf16[128,2,1024]{0,2,1:T(8,128)(2,1)}, bf16[128,2,1024]{0,2,1:T(8,128)(2,1)S(1)}, u32[]{:S(2)}, u32[]{:S(2)}) collective-permute-start(bf16[128,2,1024]{0,2,1:T(8,128)(2,1)} %get-tuple-element.99), channel_id=1, source_target_pairs={{4,0},{6,2},{8,4},{10,6},{12,8},{14,10},{16,12},{18,14},{20,16},{2... | collective-permute-start | bytes 1572872 | tf_op jit(solution)/shard_map/ppermute | solution.py:18
  225.1 42.0 %collective-permute-start.20 = (bf16[128,2,1024]{0,2,1:T(8,128)(2,1)}, bf16[128,2,1024]{0,2,1:T(8,128)(2,1)S(1)}, u32[]{:S(2)}, u32[]{:S(2)}) collective-permute-start(bf16[128,2,1024]{0,2,1:T(8,128)(2,1)} %get-tuple-element.102), channel_id=1, source_target_pairs={{0,10},{2,12},{4,14},{6,16},{8,18},{10,20},{12,22},{14,24},{16,26}... | collective-permute-start | bytes 1572872 | tf_op jit(solution)/shard_map/ppermute | solution.py:18
  232.8 21.2 %collective-permute-start.18 = (bf16[128,2,1024]{0,2,1:T(8,128)(2,1)}, bf16[128,2,1024]{0,2,1:T(8,128)(2,1)S(1)}, u32[]{:S(2)}, u32[]{:S(2)}) collective-permute-start(bf16[128,2,1024]{0,2,1:T(8,128)(2,1)} %get-tuple-element.102), channel_id=1, source_target_pairs={{8,0},{10,2},{12,4},{14,6},{16,8},{18,10},{20,12},{22,14},{24,16},... | collective-permute-start | bytes 1572872 | tf_op jit(solution)/shard_map/ppermute | solution.py:18
  235.3 12.3 %collective-permute-start.15 = (bf16[128,2,1024]{0,2,1:T(8,128)(2,1)}, bf16[128,2,1024]{0,2,1:T(8,128)(2,1)S(1)}, u32[]{:S(2)}, u32[]{:S(2)}) collective-permute-start(bf16[128,2,1024]{0,2,1:T(8,128)(2,1)} %get-tuple-element.99), channel_id=1, source_target_pairs={{0,2},{2,4},{4,6},{6,8},{8,10},{10,12},{12,14},{14,16},{16,18},{18... | collective-permute-start | bytes 1572872 | tf_op jit(solution)/shard_map/ppermute | solution.py:18
  247.6 46.2 %collective-permute-start.16 = (bf16[128,4,1024]{0,2,1:T(8,128)(2,1)}, bf16[128,4,1024]{0,2,1:T(8,128)(2,1)S(1)}, u32[]{:S(2)}, u32[]{:S(2)}) collective-permute-start(bf16[128,4,1024]{0,2,1:T(8,128)(2,1)} %get-tuple-element.45), channel_id=1, source_target_pairs={{6,0},{8,2},{10,4},{12,6},{14,8},{16,10},{18,12},{20,14},{22,16},{... | collective-permute-start | bytes 3145736 | tf_op jit(solution)/shard_map/ppermute | solution.py:18
  253.9 37.3 %collective-permute-start.17 = (bf16[128,4,1024]{0,2,1:T(8,128)(2,1)}, bf16[128,4,1024]{0,2,1:T(8,128)(2,1)}, u32[]{:S(2)}, u32[]{:S(2)}) collective-permute-start(bf16[128,4,1024]{0,2,1:T(8,128)(2,1)} %get-tuple-element.45), channel_id=1, source_target_pairs={{0,6},{2,8},{4,10},{6,12},{8,14},{10,16},{12,18},{14,20},{16,22},{... | collective-permute-start | bytes 3145736 | tf_op jit(solution)/shard_map/ppermute | solution.py:18
  263.0 24.3 %collective-permute-start.10 = (bf16[128,4,1024]{0,2,1:T(8,128)(2,1)S(1)}, bf16[128,4,1024]{0,2,1:T(8,128)(2,1)S(1)}, u32[]{:S(2)}, u32[]{:S(2)}) collective-permute-start(bf16[128,4,1024]{0,2,1:T(8,128)(2,1)S(1)} %copy-done.37), channel_id=1, source_target_pairs={{0,1},{1,0},{2,3},{3,2},{4,5},{5,4},{6,7},{7,6},{8,9},{9,8},{10,11... | collective-permute-start | bytes 3145736 | tf_op jit(solution)/shard_map/ppermute | solution.py:100
  268.3 19.1 %copy-start.31 = (bf16[4,1024,256]{2,1,0:T(8,128)(2,1)S(1)}, bf16[4,1024,256]{2,1,0:T(8,128)(2,1)}, u32[]{:S(2)}) copy-start(bf16[4,1024,256]{2,1,0:T(8,128)(2,1)} %bitcast_convert_fusion) | copy-start | bytes 6291460
  (111 other events, 559.5 us)

commit v2 on v0

--- a/solution.py
+++ b/solution.py
@@ -51,6 +51,9 @@
     count = lax.axis_size("band")
     radices = []
     rest = count
+    while rest % 4 == 0:
+        radices.append(4)
+        rest //= 4
     while rest % 2 == 0:
         radices.append(2)
         rest //= 2
@@ -189,7 +192,8 @@
             grad_input = grad_input + kernel[which, 4 + col_step][:, None, None] * jnp.roll(
                 grad_f, col_step * spacing, axis=-1
             )
-    for which, spacing in enumerate(dilations):
+    for which in (0, 2, 1):
+        spacing = dilations[which]
         grad_input = lax.optimization_barrier(grad_input)
         for row_step in (-1, 1):
             rows = grad_halo[(which, -row_step * spacing)].astype(jnp.float32)

time: 324 us -> 298 us (0.920)
  the two profiles are of different devices: /device:TPU:3 before, /device:TPU:13 now
where the time goes in v2:
time: 298 us; the launch traced here: 292 us
  starting transfers between devices  103 us (35%)
  other arithmetic  61.9 us (21%)
  local copies, waits for them, and re-layouts  55.2 us (19%)
  waiting for transfers between devices  55.1 us (18%)
  matrix products  13.4 us (4%)
  between operations  3.08 us (1%)
    ppermute x20, starting transfers between devices, shifted(): return lax.ppermute(block, axis, route)  90.4 us
    ppermute x20, waiting for transfers between devices, shifted(): return lax.ppermute(block, axis, route)  35 us
    unnamed x257, local copies, waits for them, and re-layouts  18.8 us
    reduce_sum x4, other arithmetic, block(): jnp.sum(grad_f * jnp.roll(feat_rows[row_step * spacing], -col_step * spac...  18.1 us
    another operation x3, other arithmetic, block(): stacked = jnp.stack(branches)  16 us
    ppermute x2, waiting for transfers between devices, chan_shift(): lax.ppermute(block, 'chan', [(j, (j + s) % count) for j in range(count)])  12.5 us
    slice x18, local copies, waits for them, and re-layouts, block(): jnp.roll(feat_rows[row_step * spacing], -col_step * spacing, axis=-1)  11.1 us
    ppermute x6, starting transfers between devices, band_allreduce(): got = lax.ppermute(flat, 'band', rotate(stride, radix, u))  9.98 us
  transfers between devices with their start and end apart: 34, of which 10 were waited for; matrix products, arithmetic and copies ran while one was open for 39% of the time, Pallas kernels for 0%

profile of v2, /device:TPU:13, one launch (start us, length us, event | category | flops | bytes accessed | tf_op | source)
XLA Modules:
  0.0 291.8 jit_solution(14658993318283786149)
XLA Ops:
  3.7 2.1 collective-permute-start.8
  5.7 5.0 %collective-permute-start.6 = (bf16[128,2,1024]{0,2,1:T(8,128)(2,1)}, bf16[128,2,1024]{0,2,1:T(8,128)(2,1)}, u32[]{:S(2)}, u32[]{:S(2)}) collective-permute-start(bf16[128,2,1024]{0,2,1:T(8,128)(2,1)} %get-tuple-element.123), channel_id=1, source_target_pairs={{0,10},{2,12},{4,14},{6,16},{8,18},{10,20},{12,22},{14,24},{16,26}... | collective-permute-start | bytes 1572872 | tf_op jit(solution)/shard_map/ppermute | solution.py:18
  12.6 4.0 %collective-permute-start = (bf16[128,2,1024]{0,2,1:T(8,128)(2,1)}, bf16[128,2,1024]{0,2,1:T(8,128)(2,1)}, u32[]{:S(2)}, u32[]{:S(2)}) collective-permute-start(bf16[128,2,1024]{0,2,1:T(8,128)(2,1)} %get-tuple-element.123), channel_id=1, source_target_pairs={{0,4},{2,6},{4,8},{6,10},{8,12},{10,14},{12,16},{14,18},{16,20},{1... | collective-permute-start | bytes 1572872 | tf_op jit(solution)/shard_map/ppermute | solution.py:18
  19.8 2.3 fusion.132
  22.1 2.3 fusion.128
  27.4 2.5 copy.33
  30.0 2.5 fusion.78
  32.5 4.6 %collective-permute-start.9 = (bf16[128,2,1024]{0,2,1:T(8,128)(2,1)}, bf16[128,2,1024]{0,2,1:T(8,128)(2,1)S(1)}, u32[]{:S(2)}, u32[]{:S(2)}) collective-permute-start(bf16[128,2,1024]{0,2,1:T(8,128)(2,1)} %get-tuple-element.124), channel_id=1, source_target_pairs={{10,0},{12,2},{14,4},{16,6},{18,8},{20,10},{22,12},{24,14},{26,16}... | collective-permute-start | bytes 1572872 | tf_op jit(solution)/shard_map/ppermute | solution.py:18
  37.1 9.9 %collective-permute-start.3 = (bf16[128,2,1024]{0,2,1:T(8,128)(2,1)}, bf16[128,2,1024]{0,2,1:T(8,128)(2,1)S(1)}, u32[]{:S(2)}, u32[]{:S(2)}) collective-permute-start(bf16[128,2,1024]{0,2,1:T(8,128)(2,1)} %get-tuple-element.124), channel_id=1, source_target_pairs={{4,0},{6,2},{8,4},{10,6},{12,8},{14,10},{16,12},{18,14},{20,16},{2... | collective-permute-start | bytes 1572872 | tf_op jit(solution)/shard_map/ppermute | solution.py:18
  48.4 2.2 fusion.114
  50.6 6.3 %collective-permute-start.1 = (bf16[128,2,1024]{0,2,1:T(8,128)(2,1)}, bf16[128,2,1024]{0,2,1:T(8,128)(2,1)S(1)}, u32[]{:S(2)}, u32[]{:S(2)}) collective-permute-start(bf16[128,2,1024]{0,2,1:T(8,128)(2,1)} %get-tuple-element.124), channel_id=1, source_target_pairs={{0,2},{2,4},{4,6},{6,8},{8,10},{10,12},{12,14},{14,16},{16,18},{18... | collective-permute-start | bytes 1572872 | tf_op jit(solution)/shard_map/ppermute | solution.py:18
  60.4 5.1 %collective-permute-start.4 = (bf16[128,4,1024]{0,2,1:T(8,128)(2,1)S(1)}, bf16[128,4,1024]{0,2,1:T(8,128)(2,1)S(1)}, u32[]{:S(2)}, u32[]{:S(2)}) collective-permute-start(bf16[128,4,1024]{0,2,1:T(8,128)(2,1)S(1)} %copy.25), channel_id=1, source_target_pairs={{0,6},{2,8},{4,10},{6,12},{8,14},{10,16},{12,18},{14,20},{16,22},{... | collective-permute-start | bytes 3145736 | tf_op jit(solution)/shard_map/ppermute | solution.py:18
  65.5 8.8 %collective-permute-done.3 = bf16[128,2,1024]{0,2,1:T(8,128)(2,1)S(1)} collective-permute-done((bf16[128,2,1024]{0,2,1:T(8,128)(2,1)}, bf16[128,2,1024]{0,2,1:T(8,128)(2,1)S(1)}, u32[]{:S(2)}, u32[]{:S(2)}) %collective-permute-start.3) | collective-permute-done | bytes 524320 | tf_op jit(solution)/shard_map/ppermute | solution.py:18
  76.2 12.8 %collective-permute-done.1 = bf16[128,2,1024]{0,2,1:T(8,128)(2,1)S(1)} collective-permute-done((bf16[128,2,1024]{0,2,1:T(8,128)(2,1)}, bf16[128,2,1024]{0,2,1:T(8,128)(2,1)S(1)}, u32[]{:S(2)}, u32[]{:S(2)}) %collective-permute-start.1) | collective-permute-done | bytes 524320 | tf_op jit(solution)/shard_map/ppermute | solution.py:18
  90.4 6.1 %fusion.80 = bf16[1,128,4,1024]{1,3,0,2:T(8,128)(2,1)} fusion(f32[128,4,18]{0,2,1:T(8,128)S(1)} %get-tuple-element.88, f32[128,4,1006]{0,2,1:T(8,128)S(1)} %get-tuple-element.90, f32[128]{0:T(128)S(1)} %copy-done.87, f32[128]{0:T(128)S(1)} %copy-done.89, f32[128,4,1006]{0,2,1:T(8,128)S(1)} %get-tuple-element.89, f32[128,4,18]{0,2,1:T(8,128)S(1)} %get-tuple-element.87, ...), kind=kLoop, calls=%fused_computation.168 | loop fusion | flops 15204352 | bytes 16781824 | tf_op jit(solution)/shard_map/stack | solution.py:147
  98.2 5.5 %fusion.82 = bf16[1,128,4,1024]{1,3,0,2:T(8,128)(2,1)} fusion(f32[128,4,6]{0,2,1:T(8,128)S(1)} %get-tuple-element.80, f32[128,4,1018]{0,2,1:T(8,128)S(1)} %get-tuple-element.82, f32[128]{0:T(128)S(1)} %copy-done.103, f32[128]{0:T(128)S(1)} %copy-done.105, f32[128,4,1018]{0,2,1:T(8,128)S(1)} %get-tuple-element.81, f32[128,4,6]{0,2,1:T(8,128)S(1)} %get-tuple-element.79, ...), kind=kLoop, calls=%fused_computation.170 | loop fusion | flops 15204352 | bytes 16781824 | tf_op jit(solution)/shard_map/stack | solution.py:147
  103.7 2.5 add_convert_fusion
  106.3 2.7 slice_bitcast_fusion.1
  110.1 2.5 collective-permute-start.18
  112.6 5.8 %collective-permute-start.16 = (bf16[128,2,1024]{0,2,1:T(8,128)(2,1)}, bf16[128,2,1024]{0,2,1:T(8,128)(2,1)}, u32[]{:S(2)}, u32[]{:S(2)}) collective-permute-start(bf16[128,2,1024]{0,2,1:T(8,128)(2,1)} %get-tuple-element.99), channel_id=1, source_target_pairs={{8,0},{10,2},{12,4},{14,6},{16,8},{18,10},{20,12},{22,14},{24,16},... | collective-permute-start | bytes 1572872 | tf_op jit(solution)/shard_map/ppermute | solution.py:18
  120.0 2.2 fusion.104
  122.2 2.2 fusion.106
  127.5 2.9 fusion.32
  130.5 4.4 %fusion.81 = bf16[1,128,4,1024]{1,3,0,2:T(8,128)(2,1)} fusion(f32[128,4,12]{0,2,1:T(8,128)S(1)} %get-tuple-element.116, f32[128,4,1012]{0,2,1:T(8,128)S(1)} %get-tuple-element.118, f32[128]{0:T(128)S(1)} %copy-done.75, bf16[128,4,1024]{0,2,1:T(8,128)(2,1)S(1)} %collective-permute-done.5, f32[128]{0:T(128)S(1)} %copy-done.77, f32[128,4,1012]{0,2,1:T(8,128)} %copy-done.10, ...), kind=kLoop, calls=%fused_computation.169 | loop fusion | flops 14155776 | bytes 16781824 | tf_op jit(solution)/shard_map/stack | solution.py:147
  134.9 4.0 %bitcast_convert_fusion = bf16[4,1024,256]{2,1,0:T(8,128)(2,1)} fusion(bf16[4,128,256]{2,1,0:T(8,128)(2,1)S(1)} %copy-done, bf16[1,128,4,1024]{1,3,0,2:T(8,128)(2,1)S(1)} %copy-done.33, bf16[1,128,4,1024]{1,3,0,2:T(8,128)(2,1)} %fusion.81, bf16[1,128,4,1024]{1,3,0,2:T(8,128)(2,1)S(1)} %copy-done.34, bf16[1,128,4,1024]{1,3,0,2:T(8,128)(2,1)S(1)} %bitcast.215), kind=kOutput, calls=%fused_computation.32 | convolution fusion | flops 1081081856 | bytes 6553600 | tf_op jit(solution)/shard_map/bchw,bco->ohw/dot_general | solution.py:149
  140.7 2.7 fusion.73
  144.4 4.7 %fusion.30 = (f32[128]{0:T(128)}, f32[128]{0:T(128)}, f32[128]{0:T(128)}, f32[128]{0:T(128)}, f32[128]{0:T(128)}, /*index=5*/f32[128]{0:T(128)}, f32[128]{0:T(128)}, f32[128]{0:T(128)}) fusion(bf16[128,4,1024]{0,2,1:T(8,128)(2,1)S(1)} %copy.25, bf16[4,128,4,1024]{1,3,2,0:T(8,128)(2,1)S(1)} %add_convert_fusion, f32[128,4,6]{0,2,1:T(8,128)S(1)} %copy-done.45, ...), kind=kLoop, calls=%fused_computation.66 | loop fusion | flops 13630464 | bytes 13635584 | tf_op jit(solution)/shard_map/reduce_sum | solution.py:176
  149.3 3.9 %fusion.33 = (f32[128]{0:T(128)S(1)}, f32[128]{0:T(128)S(1)}, f32[128]{0:T(128)S(1)}, f32[128]{0:T(128)S(1)}, f32[128]{0:T(128)S(1)}, /*index=5*/f32[128]{0:T(128)S(1)}, f32[128]{0:T(128)S(1)}) fusion(bf16[128,2,1024]{0,2,1:T(8,128)(2,1)S(1)} %collective-permute-done.3, bf16[128,2,1024]{0,2,1:T(8,128)(2,1)} %collective-permute-done.2, ...), kind=kLoop, calls=%fused_computation.69 | loop fusion | flops 13630592 | bytes 13635072 | tf_op jit(solution)/shard_map/reduce_sum | solution.py:176
  153.4 6.5 %fusion.34 = (f32[128]{0:T(128)S(1)}, f32[128]{0:T(128)S(1)}, f32[128]{0:T(128)S(1)}, f32[128]{0:T(128)S(1)}, f32[128]{0:T(128)S(1)}, /*index=5*/f32[128]{0:T(128)S(1)}) fusion(f32[128,4,6]{0,2,1:T(8,128)S(1)} %copy-done.47, f32[128,4,1018]{0,2,1:T(8,128)} %copy-done.7, bf16[4,128,4,1024]{1,3,2,0:T(8,128)(2,1)} %copy-done.2, ...), kind=kLoop, calls=%fused_computation.70 | loop fusion | flops 11009280 | bytes 13634560 | tf_op jit(solution)/shard_map/reduce_sum | solution.py:176
  167.3 3.4 %collective-permute-done.24 = f32[33632]{0:T(1024)S(1)} collective-permute-done((f32[33632]{0:T(1024)S(1)}, f32[33632]{0:T(1024)S(1)}, u32[]{:S(2)}, u32[]{:S(2)}) %collective-permute-start.24) | collective-permute-done | bytes 134560 | tf_op jit(solution)/shard_map/ppermute | solution.py:83
  173.6 4.6 %fusion.25 = f32[128,4,1024]{0,2,1:T(8,128)} fusion(f32[128,4,6]{0,2,1:T(8,128)S(1)} %get-tuple-element.72, f32[128,4,1018]{0,2,1:T(8,128)S(1)} %get-tuple-element.74, f32[128,4,1018]{0,2,1:T(8,128)S(1)} %get-tuple-element.73, f32[128,4,6]{0,2,1:T(8,128)S(1)} %get-tuple-element.71, f32[128,4,12]{0,2,1:T(8,128)S(1)} %copy-done.55, ...), kind=kLoop, calls=%fused_computation.61 | loop fusion | flops 14680064 | bytes 18878976 | tf_op jit(solution)/shard_map/add | solution.py:192
  178.6 2.4 collective-permute-start.29
  185.5 4.4 %collective-permute-start.33 = (f32[33632]{0:T(1024)S(1)}, f32[33632]{0:T(1024)S(1)}, u32[]{:S(2)}, u32[]{:S(2)}) collective-permute-start(f32[33632]{0:T(1024)S(1)} %dynamic_update_slice.35), channel_id=1, source_target_pairs={{0,6},{2,0},{4,2},{6,4},{8,14},{10,8},{12,10},{14,12},{16,22},{18,... | collective-permute-start | bytes 403592 | tf_op jit(solution)/shard_map/ppermute | solution.py:92
  194.1 2.4 collective-permute-done.31
  196.4 3.1 %collective-permute-start.19 = (bf16[128,2,1024]{0,2,1:T(8,128)(2,1)}, bf16[128,2,1024]{0,2,1:T(8,128)(2,1)}, u32[]{:S(2)}, u32[]{:S(2)}) collective-permute-start(bf16[128,2,1024]{0,2,1:T(8,128)(2,1)} %get-tuple-element.100), channel_id=1, source_target_pairs={{0,8},{2,10},{4,12},{6,14},{8,16},{10,18},{12,20},{14,22},{16,24},... | collective-permute-start | bytes 1572872 | tf_op jit(solution)/shard_map/ppermute | solution.py:18
  200.8 5.4 %collective-permute-start.17 = (bf16[128,2,1024]{0,2,1:T(8,128)(2,1)}, bf16[128,2,1024]{0,2,1:T(8,128)(2,1)S(1)}, u32[]{:S(2)}, u32[]{:S(2)}) collective-permute-start(bf16[128,2,1024]{0,2,1:T(8,128)(2,1)} %get-tuple-element.100), channel_id=1, source_target_pairs={{10,0},{12,2},{14,4},{16,6},{18,8},{20,10},{22,12},{24,14},{26,16}... | collective-permute-start | bytes 1572872 | tf_op jit(solution)/shard_map/ppermute | solution.py:18
  208.2 2.9 collective-permute-start.14
  215.9 6.1 %collective-permute-done.17 = bf16[128,2,1024]{0,2,1:T(8,128)(2,1)S(1)} collective-permute-done((bf16[128,2,1024]{0,2,1:T(8,128)(2,1)}, bf16[128,2,1024]{0,2,1:T(8,128)(2,1)S(1)}, u32[]{:S(2)}, u32[]{:S(2)}) %collective-permute-start.17) | collective-permute-done | bytes 524320 | tf_op jit(solution)/shard_map/ppermute | solution.py:18
  225.4 5.0 %collective-permute-done.14 = bf16[128,2,1024]{0,2,1:T(8,128)(2,1)S(1)} collective-permute-done((bf16[128,2,1024]{0,2,1:T(8,128)(2,1)}, bf16[128,2,1024]{0,2,1:T(8,128)(2,1)S(1)}, u32[]{:S(2)}, u32[]{:S(2)}) %collective-permute-start.14) | collective-permute-done | bytes 524320 | tf_op jit(solution)/shard_map/ppermute | solution.py:18
  230.4 3.4 %collective-permute-start.13 = (bf16[128,2,1024]{0,2,1:T(8,128)(2,1)}, bf16[128,2,1024]{0,2,1:T(8,128)(2,1)S(1)}, u32[]{:S(2)}, u32[]{:S(2)}) collective-permute-start(bf16[128,2,1024]{0,2,1:T(8,128)(2,1)} %get-tuple-element.102), channel_id=1, source_target_pairs={{4,0},{6,2},{8,4},{10,6},{12,8},{14,10},{16,12},{18,14},{20,16},{2... | collective-permute-start | bytes 1572872 | tf_op jit(solution)/shard_map/ppermute | solution.py:18
  233.8 2.3 collective-permute-done.15
  236.1 18.7 %collective-permute-start.20 = (bf16[128,4,1024]{0,2,1:T(8,128)(2,1)}, bf16[128,4,1024]{0,2,1:T(8,128)(2,1)S(1)}, u32[]{:S(2)}, u32[]{:S(2)}) collective-permute-start(bf16[128,4,1024]{0,2,1:T(8,128)(2,1)} %get-tuple-element.41), channel_id=1, source_target_pairs={{6,0},{8,2},{10,4},{12,6},{14,8},{16,10},{18,12},{20,14},{22,16},{... | collective-permute-start | bytes 3145736 | tf_op jit(solution)/shard_map/ppermute | solution.py:18
  256.3 2.1 collective-permute-start.21
  261.2 2.6 fusion.59
  264.9 4.8 %fusion.65 = f32[128,4,1024]{0,2,1:T(8,128)} fusion(f32[128,4,1024]{0,2,1:T(8,128)S(1)} %fusion.59, f32[128,4,18]{0,2,1:T(8,128)S(1)} %get-tuple-element.52, f32[128,4,1006]{0,2,1:T(8,128)S(1)} %get-tuple-element.54, f32[128,4,1006]{0,2,1:T(8,128)S(1)} %get-tuple-element.53, f32[128,4,18]{0,2,1:T(8,128)S(1)} %get-tuple-element.51, ...), kind=kLoop, calls=%fused_computation.130 | loop fusion | flops 10485760 | bytes 14683136 | tf_op jit(solution)/shard_map/add | solution.py:202
  269.7 12.5 %collective-permute-done.10 = bf16[128,4,1024]{0,2,1:T(8,128)(2,1)S(1)} collective-permute-done((bf16[128,4,1024]{0,2,1:T(8,128)(2,1)S(1)}, bf16[128,4,1024]{0,2,1:T(8,128)(2,1)S(1)}, u32[]{:S(2)}, u32[]{:S(2)}) %collective-permute-start.10) | collective-permute-done | bytes 1048608 | tf_op jit(solution)/shard_map/ppermute | solution.py:100
  286.1 2.5 fusion.71
  288.6 3.0 %copy.41 = f32[128,4,1024]{2,1,0:T(4,128)} copy(f32[128,4,1024]{0,2,1:T(8,128)} %fusion.71) | data formatting | bytes 4194304
  (371 shorter events, 68.1 us)
Async XLA Ops:
  0.6 29.3 %copy-start = (bf16[4,128,256]{2,1,0:T(8,128)(2,1)S(1)}, bf16[4,128,256]{2,1,0:T(8,128)(2,1)}, u32[]{:S(2)}) copy-start(bf16[4,128,256]{2,1,0:T(8,128)(2,1)} %param.6) | copy-start | bytes 786436
  3.7 46.9 %collective-permute-start.8 = (bf16[128,2,1024]{0,2,1:T(8,128)(2,1)}, bf16[128,2,1024]{0,2,1:T(8,128)(2,1)}, u32[]{:S(2)}, u32[]{:S(2)}) collective-permute-start(bf16[128,2,1024]{0,2,1:T(8,128)(2,1)} %get-tuple-element.123), channel_id=1, source_target_pairs={{8,0},{10,2},{12,4},{14,6},{16,8},{18,10},{20,12},{22,14},{24,16},... | collective-permute-start | bytes 1572872 | tf_op jit(solution)/shard_map/ppermute | solution.py:18
  5.7 26.7 %collective-permute-start.6 = (bf16[128,2,1024]{0,2,1:T(8,128)(2,1)}, bf16[128,2,1024]{0,2,1:T(8,128)(2,1)}, u32[]{:S(2)}, u32[]{:S(2)}) collective-permute-start(bf16[128,2,1024]{0,2,1:T(8,128)(2,1)} %get-tuple-element.123), channel_id=1, source_target_pairs={{0,10},{2,12},{4,14},{6,16},{8,18},{10,20},{12,22},{14,24},{16,26}... | collective-permute-start | bytes 1572872 | tf_op jit(solution)/shard_map/ppermute | solution.py:18
  10.7 49.7 %collective-permute-start.2 = (bf16[128,2,1024]{0,2,1:T(8,128)(2,1)}, bf16[128,2,1024]{0,2,1:T(8,128)(2,1)}, u32[]{:S(2)}, u32[]{:S(2)}) collective-permute-start(bf16[128,2,1024]{0,2,1:T(8,128)(2,1)} %get-tuple-element.123), channel_id=1, source_target_pairs={{2,0},{4,2},{6,4},{8,6},{10,8},{12,10},{14,12},{16,14},{18,16},{20... | collective-permute-start | bytes 1572872 | tf_op jit(solution)/shard_map/ppermute | solution.py:18
  12.6 63.5 %collective-permute-start = (bf16[128,2,1024]{0,2,1:T(8,128)(2,1)}, bf16[128,2,1024]{0,2,1:T(8,128)(2,1)}, u32[]{:S(2)}, u32[]{:S(2)}) collective-permute-start(bf16[128,2,1024]{0,2,1:T(8,128)(2,1)} %get-tuple-element.123), channel_id=1, source_target_pairs={{0,4},{2,6},{4,8},{6,10},{8,12},{10,14},{12,16},{14,18},{16,20},{1... | collective-permute-start | bytes 1572872 | tf_op jit(solution)/shard_map/ppermute | solution.py:18
  16.6 20.5 %collective-permute-start.7 = (bf16[128,2,1024]{0,2,1:T(8,128)(2,1)}, bf16[128,2,1024]{0,2,1:T(8,128)(2,1)}, u32[]{:S(2)}, u32[]{:S(2)}) collective-permute-start(bf16[128,2,1024]{0,2,1:T(8,128)(2,1)} %get-tuple-element.124), channel_id=1, source_target_pairs={{0,8},{2,10},{4,12},{6,14},{8,16},{10,18},{12,20},{14,22},{16,24},... | collective-permute-start | bytes 1572872 | tf_op jit(solution)/shard_map/ppermute | solution.py:18
  26.0 70.9 %copy-start.4 = (f32[128,4,1018]{0,2,1:T(8,128)}, f32[128,4,1018]{0,2,1:T(8,128)S(1)}, u32[]{:S(2)}) copy-start(f32[128,4,1018]{0,2,1:T(8,128)S(1)} %get-tuple-element.105) | copy-start | bytes 6254596
  32.5 24.5 %collective-permute-start.9 = (bf16[128,2,1024]{0,2,1:T(8,128)(2,1)}, bf16[128,2,1024]{0,2,1:T(8,128)(2,1)S(1)}, u32[]{:S(2)}, u32[]{:S(2)}) collective-permute-start(bf16[128,2,1024]{0,2,1:T(8,128)(2,1)} %get-tuple-element.124), channel_id=1, source_target_pairs={{10,0},{12,2},{14,4},{16,6},{18,8},{20,10},{22,12},{24,14},{26,16}... | collective-permute-start | bytes 1572872 | tf_op jit(solution)/shard_map/ppermute | solution.py:18
  37.1 37.2 %collective-permute-start.3 = (bf16[128,2,1024]{0,2,1:T(8,128)(2,1)}, bf16[128,2,1024]{0,2,1:T(8,128)(2,1)S(1)}, u32[]{:S(2)}, u32[]{:S(2)}) collective-permute-start(bf16[128,2,1024]{0,2,1:T(8,128)(2,1)} %get-tuple-element.124), channel_id=1, source_target_pairs={{4,0},{6,2},{8,4},{10,6},{12,8},{14,10},{16,12},{18,14},{20,16},{2... | collective-permute-start | bytes 1572872 | tf_op jit(solution)/shard_map/ppermute | solution.py:18
  50.6 38.4 %collective-permute-start.1 = (bf16[128,2,1024]{0,2,1:T(8,128)(2,1)}, bf16[128,2,1024]{0,2,1:T(8,128)(2,1)S(1)}, u32[]{:S(2)}, u32[]{:S(2)}) collective-permute-start(bf16[128,2,1024]{0,2,1:T(8,128)(2,1)} %get-tuple-element.124), channel_id=1, source_target_pairs={{0,2},{2,4},{4,6},{6,8},{8,10},{10,12},{12,14},{14,16},{16,18},{18... | collective-permute-start | bytes 1572872 | tf_op jit(solution)/shard_map/ppermute | solution.py:18
  57.0 33.3 %copy-start.22 = (bf16[128,2,1024]{0,2,1:T(8,128)(2,1)}, bf16[128,2,1024]{0,2,1:T(8,128)(2,1)S(1)}, u32[]{:S(2)}) copy-start(bf16[128,2,1024]{0,2,1:T(8,128)(2,1)S(1)} %collective-permute-done.9) | copy-start | bytes 1572868
  57.0 67.5 %collective-permute-start.5 = (bf16[128,4,1024]{0,2,1:T(8,128)(2,1)S(1)}, bf16[128,4,1024]{0,2,1:T(8,128)(2,1)S(1)}, u32[]{:S(2)}, u32[]{:S(2)}) collective-permute-start(bf16[128,4,1024]{0,2,1:T(8,128)(2,1)S(1)} %copy.25), channel_id=1, source_target_pairs={{6,0},{8,2},{10,4},{12,6},{14,8},{16,10},{18,12},{20,14},{22,16},{... | collective-permute-start | bytes 3145736 | tf_op jit(solution)/shard_map/ppermute | solution.py:18
  60.1 30.1 %copy-start.38 = (f32[128,4,18]{0,2,1:T(8,128)}, f32[128,4,18]{0,2,1:T(8,128)S(1)}, u32[]{:S(2)}) copy-start(f32[128,4,18]{0,2,1:T(8,128)S(1)} %get-tuple-element.88) | copy-start | bytes 110596
  60.4 29.8 %copy-start.13 = (f32[128,4,1006]{0,2,1:T(8,128)}, f32[128,4,1006]{0,2,1:T(8,128)S(1)}, u32[]{:S(2)}) copy-start(f32[128,4,1006]{0,2,1:T(8,128)S(1)} %get-tuple-element.89) | copy-start | bytes 6180868
  60.4 29.8 %copy-start.14 = (f32[128,4,1006]{0,2,1:T(8,128)}, f32[128,4,1006]{0,2,1:T(8,128)S(1)}, u32[]{:S(2)}) copy-start(f32[128,4,1006]{0,2,1:T(8,128)S(1)} %get-tuple-element.90) | copy-start | bytes 6180868
  60.4 58.6 %collective-permute-start.4 = (bf16[128,4,1024]{0,2,1:T(8,128)(2,1)S(1)}, bf16[128,4,1024]{0,2,1:T(8,128)(2,1)S(1)}, u32[]{:S(2)}, u32[]{:S(2)}) collective-permute-start(bf16[128,4,1024]{0,2,1:T(8,128)(2,1)S(1)} %copy.25), channel_id=1, source_target_pairs={{0,6},{2,8},{4,10},{6,12},{8,14},{10,16},{12,18},{14,20},{16,22},{... | collective-permute-start | bytes 3145736 | tf_op jit(solution)/shard_map/ppermute | solution.py:18
  74.3 29.4 %collective-permute-start.11 = (bf16[128,4,1024]{2,0,1:T(8,128)(2,1)}, bf16[128,4,1024]{2,0,1:T(8,128)(2,1)}, u32[]{:S(2)}, u32[]{:S(2)}) collective-permute-start(bf16[128,4,1024]{2,0,1:T(8,128)(2,1)} %copy.33), channel_id=1, source_target_pairs={{0,1},{1,0},{2,3},{3,2},{4,5},{5,4},{6,7},{7,6},{8,9},{9,8},{10,11... | collective-permute-start | bytes 3145736 | tf_op jit(solution)/shard_map/ppermute | solution.py:100
  75.8 21.1 %copy-start.46 = (f32[128,4,6]{0,2,1:T(8,128)}, f32[128,4,6]{0,2,1:T(8,128)S(1)}, u32[]{:S(2)}) copy-start(f32[128,4,6]{0,2,1:T(8,128)S(1)} %get-tuple-element.80) | copy-start | bytes 36868
  75.8 21.1 %copy-start.52 = (f32[128,4,6]{0,2,1:T(8,128)}, f32[128,4,6]{0,2,1:T(8,128)S(1)}, u32[]{:S(2)}) copy-start(f32[128,4,6]{0,2,1:T(8,128)S(1)} %get-tuple-element.79) | copy-start | bytes 36868
  75.8 14.5 %copy-start.12 = (f32[128,4,1006]{0,2,1:T(8,128)S(1)}, f32[128,4,1006]{0,2,1:T(8,128)}, u32[]{:S(2)}) copy-start(f32[128,4,1006]{0,2,1:T(8,128)} %get-tuple-element.122) | copy-start | bytes 6180868
  76.1 20.8 %copy-start.7 = (f32[128,4,1018]{0,2,1:T(8,128)}, f32[128,4,1018]{0,2,1:T(8,128)S(1)}, u32[]{:S(2)}) copy-start(f32[128,4,1018]{0,2,1:T(8,128)S(1)} %get-tuple-element.82) | copy-start | bytes 6254596
  76.1 14.2 %copy-start.11 = (f32[128,4,1006]{0,2,1:T(8,128)S(1)}, f32[128,4,1006]{0,2,1:T(8,128)}, u32[]{:S(2)}) copy-start(f32[128,4,1006]{0,2,1:T(8,128)} %get-tuple-element.121) | copy-start | bytes 6180868
  76.1 14.2 %copy-start.57 = (f32[128]{0:T(128)S(1)}, f32[128]{0:T(128)}, u32[]{:S(2)}) copy-start(f32[128]{0:T(128)} %get-tuple-element.135) | copy-start | bytes 1540
  106.3 42.9 %copy-start.2 = (bf16[4,128,4,1024]{1,3,2,0:T(8,128)(2,1)}, bf16[4,128,4,1024]{1,3,2,0:T(8,128)(2,1)S(1)}, u32[]{:S(2)}) copy-start(bf16[4,128,4,1024]{1,3,2,0:T(8,128)(2,1)S(1)} %add_convert_fusion) | copy-start | bytes 12582916
  110.1 149.2 %collective-permute-start.18 = (bf16[128,2,1024]{0,2,1:T(8,128)(2,1)}, bf16[128,2,1024]{0,2,1:T(8,128)(2,1)}, u32[]{:S(2)}, u32[]{:S(2)}) collective-permute-start(bf16[128,2,1024]{0,2,1:T(8,128)(2,1)} %get-tuple-element.99), channel_id=1, source_target_pairs={{0,10},{2,12},{4,14},{6,16},{8,18},{10,20},{12,22},{14,24},{16,26}... | collective-permute-start | bytes 1572872 | tf_op jit(solution)/shard_map/ppermute | solution.py:18
  112.6 101.4 %collective-permute-start.16 = (bf16[128,2,1024]{0,2,1:T(8,128)(2,1)}, bf16[128,2,1024]{0,2,1:T(8,128)(2,1)}, u32[]{:S(2)}, u32[]{:S(2)}) collective-permute-start(bf16[128,2,1024]{0,2,1:T(8,128)(2,1)} %get-tuple-element.99), channel_id=1, source_target_pairs={{8,0},{10,2},{12,4},{14,6},{16,8},{18,10},{20,12},{22,14},{24,16},... | collective-permute-start | bytes 1572872 | tf_op jit(solution)/shard_map/ppermute | solution.py:18
  164.7 2.6 collective-permute-start.22
  164.8 6.0 %collective-permute-start.24 = (f32[33632]{0:T(1024)S(1)}, f32[33632]{0:T(1024)S(1)}, u32[]{:S(2)}, u32[]{:S(2)}) collective-permute-start(f32[33632]{0:T(1024)S(1)} %get-tuple-element.126), channel_id=1, source_target_pairs={{0,6},{2,0},{4,2},{6,4},{8,14},{10,8},{12,10},{14,12},{16,22},{18,... | collective-permute-start | bytes 403592 | tf_op jit(solution)/shard_map/ppermute | solution.py:83
  165.4 5.3 %collective-permute-start.23 = (f32[33632]{0:T(1024)S(1)}, f32[33632]{0:T(1024)S(1)}, u32[]{:S(2)}, u32[]{:S(2)}) collective-permute-start(f32[33632]{0:T(1024)S(1)} %get-tuple-element.127), channel_id=1, source_target_pairs={{0,4},{2,6},{4,0},{6,2},{8,12},{10,14},{12,8},{14,10},{16,20},{18,... | collective-permute-start | bytes 403592 | tf_op jit(solution)/shard_map/ppermute | solution.py:83
  171.9 6.3 %collective-permute-start.25 = (f32[8408]{0:T(1024)S(1)}, f32[8408]{0:T(1024)S(1)}, u32[]{:S(2)}, u32[]{:S(2)}) collective-permute-start(f32[8408]{0:T(1024)S(1)} %get-tuple-element.128), channel_id=1, source_target_pairs={{0,8},{2,10},{4,12},{6,14},{8,16},{10,18},{12,20},{14,22},{16,24},... | collective-permute-start | bytes 100904 | tf_op jit(solution)/shard_map/ppermute | solution.py:83
  171.9 6.3 %collective-permute-start.27 = (f32[8408]{0:T(1024)S(1)}, f32[8408]{0:T(1024)S(1)}, u32[]{:S(2)}, u32[]{:S(2)}) collective-permute-start(f32[8408]{0:T(1024)S(1)} %get-tuple-element.129), channel_id=1, source_target_pairs={{0,24},{2,26},{4,28},{6,30},{8,0},{10,2},{12,4},{14,6},{16,8},{18,... | collective-permute-start | bytes 100904 | tf_op jit(solution)/shard_map/ppermute | solution.py:83
  173.4 4.8 %collective-permute-start.26 = (f32[8408]{0:T(1024)S(1)}, f32[8408]{0:T(1024)S(1)}, u32[]{:S(2)}, u32[]{:S(2)}) collective-permute-start(f32[8408]{0:T(1024)S(1)} %get-tuple-element.130), channel_id=1, source_target_pairs={{0,16},{2,18},{4,20},{6,22},{8,24},{10,26},{12,28},{14,30},{16,0},... | collective-permute-start | bytes 100904 | tf_op jit(solution)/shard_map/ppermute | solution.py:83
  178.6 5.9 %collective-permute-start.29 = (f32[8408]{0:T(1024)S(1)}, f32[8408]{0:T(1024)S(1)}, u32[]{:S(2)}, u32[]{:S(2)}) collective-permute-start(f32[8408]{0:T(1024)S(1)} %get-tuple-element.40), channel_id=1, source_target_pairs={{0,16},{2,18},{4,20},{6,22},{8,24},{10,26},{12,28},{14,30},{16,0},... | collective-permute-start | bytes 100904 | tf_op jit(solution)/shard_map/ppermute | solution.py:92
  181.0 2.9 %collective-permute-start.28 = (f32[8408]{0:T(1024)S(1)}, f32[8408]{0:T(1024)S(1)}, u32[]{:S(2)}, u32[]{:S(2)}) collective-permute-start(f32[8408]{0:T(1024)S(1)} %get-tuple-element.40), channel_id=1, source_target_pairs={{0,8},{2,10},{4,12},{6,14},{8,16},{10,18},{12,20},{14,22},{16,24},... | collective-permute-start | bytes 100904 | tf_op jit(solution)/shard_map/ppermute | solution.py:92
  181.0 3.9 %collective-permute-start.30 = (f32[8408]{0:T(1024)S(1)}, f32[8408]{0:T(1024)S(1)}, u32[]{:S(2)}, u32[]{:S(2)}) collective-permute-start(f32[8408]{0:T(1024)S(1)} %get-tuple-element.40), channel_id=1, source_target_pairs={{0,24},{2,26},{4,28},{6,30},{8,0},{10,2},{12,4},{14,6},{16,8},{18,... | collective-permute-start | bytes 100904 | tf_op jit(solution)/shard_map/ppermute | solution.py:92
  185.5 22.7 %collective-permute-start.33 = (f32[33632]{0:T(1024)S(1)}, f32[33632]{0:T(1024)S(1)}, u32[]{:S(2)}, u32[]{:S(2)}) collective-permute-start(f32[33632]{0:T(1024)S(1)} %dynamic_update_slice.35), channel_id=1, source_target_pairs={{0,6},{2,0},{4,2},{6,4},{8,14},{10,8},{12,10},{14,12},{16,22},{18,... | collective-permute-start | bytes 403592 | tf_op jit(solution)/shard_map/ppermute | solution.py:92
  189.9 10.8 %collective-permute-start.32 = (f32[33632]{0:T(1024)S(1)}, f32[33632]{0:T(1024)}, u32[]{:S(2)}, u32[]{:S(2)}) collective-permute-start(f32[33632]{0:T(1024)S(1)} %dynamic_update_slice.35), channel_id=1, source_target_pairs={{0,4},{2,6},{4,0},{6,2},{8,12},{10,14},{12,8},{14,10},{16,20},{18,... | collective-permute-start | bytes 403592 | tf_op jit(solution)/shard_map/ppermute | solution.py:92
  190.9 5.5 %collective-permute-start.31 = (f32[33632]{0:T(1024)S(1)}, f32[33632]{0:T(1024)S(1)}, u32[]{:S(2)}, u32[]{:S(2)}) collective-permute-start(f32[33632]{0:T(1024)S(1)} %dynamic_update_slice.35), channel_id=1, source_target_pairs={{0,2},{2,4},{4,6},{6,0},{8,10},{10,12},{12,14},{14,8},{16,18},{18,... | collective-permute-start | bytes 403592 | tf_op jit(solution)/shard_map/ppermute | solution.py:92
  196.4 62.9 %collective-permute-start.19 = (bf16[128,2,1024]{0,2,1:T(8,128)(2,1)}, bf16[128,2,1024]{0,2,1:T(8,128)(2,1)}, u32[]{:S(2)}, u32[]{:S(2)}) collective-permute-start(bf16[128,2,1024]{0,2,1:T(8,128)(2,1)} %get-tuple-element.100), channel_id=1, source_target_pairs={{0,8},{2,10},{4,12},{6,14},{8,16},{10,18},{12,20},{14,22},{16,24},... | collective-permute-start | bytes 1572872 | tf_op jit(solution)/shard_map/ppermute | solution.py:18
  200.8 21.2 %collective-permute-start.17 = (bf16[128,2,1024]{0,2,1:T(8,128)(2,1)}, bf16[128,2,1024]{0,2,1:T(8,128)(2,1)S(1)}, u32[]{:S(2)}, u32[]{:S(2)}) collective-permute-start(bf16[128,2,1024]{0,2,1:T(8,128)(2,1)} %get-tuple-element.100), channel_id=1, source_target_pairs={{10,0},{12,2},{14,4},{16,6},{18,8},{20,10},{22,12},{24,14},{26,16}... | collective-permute-start | bytes 1572872 | tf_op jit(solution)/shard_map/ppermute | solution.py:18
  208.2 22.1 %collective-permute-start.14 = (bf16[128,2,1024]{0,2,1:T(8,128)(2,1)}, bf16[128,2,1024]{0,2,1:T(8,128)(2,1)S(1)}, u32[]{:S(2)}, u32[]{:S(2)}) collective-permute-start(bf16[128,2,1024]{0,2,1:T(8,128)(2,1)} %get-tuple-element.101), channel_id=1, source_target_pairs={{0,4},{2,6},{4,8},{6,10},{8,12},{10,14},{12,16},{14,18},{16,20},{1... | collective-permute-start | bytes 1572872 | tf_op jit(solution)/shard_map/ppermute | solution.py:18
  214.0 42.3 %collective-permute-start.12 = (bf16[128,2,1024]{0,2,1:T(8,128)(2,1)}, bf16[128,2,1024]{0,2,1:T(8,128)(2,1)S(1)}, u32[]{:S(2)}, u32[]{:S(2)}) collective-permute-start(bf16[128,2,1024]{0,2,1:T(8,128)(2,1)} %get-tuple-element.101), channel_id=1, source_target_pairs={{2,0},{4,2},{6,4},{8,6},{10,8},{12,10},{14,12},{16,14},{18,16},{20... | collective-permute-start | bytes 1572872 | tf_op jit(solution)/shard_map/ppermute | solution.py:18
  222.0 14.1 %collective-permute-start.15 = (bf16[128,2,1024]{0,2,1:T(8,128)(2,1)}, bf16[128,2,1024]{0,2,1:T(8,128)(2,1)S(1)}, u32[]{:S(2)}, u32[]{:S(2)}) collective-permute-start(bf16[128,2,1024]{0,2,1:T(8,128)(2,1)} %get-tuple-element.102), channel_id=1, source_target_pairs={{0,2},{2,4},{4,6},{6,8},{8,10},{10,12},{12,14},{14,16},{16,18},{18... | collective-permute-start | bytes 1572872 | tf_op jit(solution)/shard_map/ppermute | solution.py:18
  230.4 28.1 %collective-permute-start.13 = (bf16[128,2,1024]{0,2,1:T(8,128)(2,1)}, bf16[128,2,1024]{0,2,1:T(8,128)(2,1)S(1)}, u32[]{:S(2)}, u32[]{:S(2)}) collective-permute-start(bf16[128,2,1024]{0,2,1:T(8,128)(2,1)} %get-tuple-element.102), channel_id=1, source_target_pairs={{4,0},{6,2},{8,4},{10,6},{12,8},{14,10},{16,12},{18,14},{20,16},{2... | collective-permute-start | bytes 1572872 | tf_op jit(solution)/shard_map/ppermute | solution.py:18
  236.1 48.4 %collective-permute-start.20 = (bf16[128,4,1024]{0,2,1:T(8,128)(2,1)}, bf16[128,4,1024]{0,2,1:T(8,128)(2,1)S(1)}, u32[]{:S(2)}, u32[]{:S(2)}) collective-permute-start(bf16[128,4,1024]{0,2,1:T(8,128)(2,1)} %get-tuple-element.41), channel_id=1, source_target_pairs={{6,0},{8,2},{10,4},{12,6},{14,8},{16,10},{18,12},{20,14},{22,16},{... | collective-permute-start | bytes 3145736 | tf_op jit(solution)/shard_map/ppermute | solution.py:18
  256.3 27.9 %collective-permute-start.21 = (bf16[128,4,1024]{0,2,1:T(8,128)(2,1)}, bf16[128,4,1024]{0,2,1:T(8,128)(2,1)S(1)}, u32[]{:S(2)}, u32[]{:S(2)}) collective-permute-start(bf16[128,4,1024]{0,2,1:T(8,128)(2,1)} %get-tuple-element.41), channel_id=1, source_target_pairs={{0,6},{2,8},{4,10},{6,12},{8,14},{10,16},{12,18},{14,20},{16,22},{... | collective-permute-start | bytes 3145736 | tf_op jit(solution)/shard_map/ppermute | solution.py:18
  258.4 23.7 %collective-permute-start.10 = (bf16[128,4,1024]{0,2,1:T(8,128)(2,1)S(1)}, bf16[128,4,1024]{0,2,1:T(8,128)(2,1)S(1)}, u32[]{:S(2)}, u32[]{:S(2)}) collective-permute-start(bf16[128,4,1024]{0,2,1:T(8,128)(2,1)S(1)} %copy-done.37), channel_id=1, source_target_pairs={{0,1},{1,0},{2,3},{3,2},{4,5},{5,4},{6,7},{7,6},{8,9},{9,8},{10,11... | collective-permute-start | bytes 3145736 | tf_op jit(solution)/shard_map/ppermute | solution.py:100
  264.9 17.3 %copy-start.27 = (bf16[4,1024,256]{2,1,0:T(8,128)(2,1)S(1)}, bf16[4,1024,256]{2,1,0:T(8,128)(2,1)}, u32[]{:S(2)}) copy-start(bf16[4,1024,256]{2,1,0:T(8,128)(2,1)} %bitcast_convert_fusion) | copy-start | bytes 6291460
  (111 other events, 543.8 us)
